TPU v7x, 256 devices: a whole 4x4x8 slice. The times are simulated.
256 devices in a mesh: band: 16 (over z_hi, y, core), grid: 16 (over x, z_lo).
Axes of the slice: x: 4, y: 4, z: 8 (z_hi: 2, z_lo: 4; z = z_hi * 4 + z_lo), core: 2. Of those that a mesh axis runs over, the one named last changes fastest.
Arguments:
- bands: float32 [16, 2, 128, 128, 128], P('band', None, 'grid'), may hold values from -6 to 6
- coulomb: float32 [128, 128, 128], P(None, 'grid'), may hold values from 0.1 to 10
Outputs:
- exchange: float32 [16, 2, 128, 128, 128], P('band', None, 'grid')
All inputs are finite; a program needn't handle non-finite values.
Results may differ from a plain program's by a relative error of at most 0.0001.
Values sent between devices are 32-bit elements; how exact they have to be, the bound alone decides.
No kernel may reach another device: no remote copies, remote signals or barrier semaphores. Data moves between devices by JAX's collectives and lax.ppermute only.
A program may use at most 64 MiB of HBM per device.

v0:
```python
import math

import jax
import jax.numpy as jnp
from jax import lax
from jax.sharding import PartitionSpec as P

NX = 128
NY = 128
NZ = 128
STEPS = 2


fused_forms = {1: "prnbc,rntk->ptkbc", 2: "pranc,rntk->ptakc", 3: "prabn,rntk->ptabk"}


def band_place(half, row, core):
    return half * 8 + row * 2 + core


def half_tree(value, axis):
    def send(operand, pairs):
        return lax.ppermute(operand, axis, [(band_place(h, *a), band_place(h, *b)) for h in (0, 1) for a, b in pairs])

    first = [send(value, [((0, 0), (0, 1))]), send(value, [((0, 0), (1, 0))]), send(value, [((0, 0), (3, 0))])]
    relay = first[1] + first[2]
    second = [
        send(relay, [((1, 0), (1, 1)), ((3, 0), (3, 1))]),
        send(relay, [((1, 0), (2, 0))]),
        send(relay, [((3, 0), (2, 1))]),
    ]
    total = first[0] + relay
    for part in second:
        total = total + part
    return total


def visitors_of(bands, axis):
    index = lax.axis_index(axis)
    head = index % 8 == 0
    own = jnp.where(head, bands, 0).astype(bands.dtype)
    crossed = lax.ppermute(bands, axis, [(0, 8), (8, 0)])
    return [own + half_tree(own, axis), crossed + half_tree(crossed, axis)]


def dft_tables(length):
    indices = jnp.arange(length, dtype=jnp.int32)
    products = indices[:, None] * indices[None, :] % length
    angles = products.astype(jnp.float32) * (2.0 * math.pi / length)
    return (jnp.cos(angles), jnp.sin(angles))


def transform(real_part, imag_part, axis_dim, inverse):
    cosine, sine_table = dft_tables(real_part.shape[axis_dim])
    signed = -sine_table if inverse else sine_table
    table = jnp.stack([jnp.stack([cosine, -signed], 1), jnp.stack([signed, cosine], 1)], 0)
    values = jnp.stack([real_part, imag_part], axis=1)
    out = jnp.einsum(fused_forms[axis_dim], values, table, precision=lax.Precision.HIGH)
    return (out[:, 0], out[:, 1])


def body(bands, coulomb):
    local = bands.shape[0]
    kernel = coulomb * (1.0 / (NX * NY * NZ))
    own_re = bands[:, 0]
    own_im = bands[:, 1]
    totals = (jnp.zeros_like(own_re), jnp.zeros_like(own_im))
    for visit_index, visitors in enumerate(visitors_of(bands, "band")):
        if visit_index:
            own, visitors = lax.optimization_barrier((bands, visitors))
            own_re = own[:, 0]
            own_im = own[:, 1]
        pair_vis_re = visitors[:, 0]
        pair_vis_im = visitors[:, 1]
        pair_real_part = pair_vis_re[None] * own_re[:, None] + pair_vis_im[None] * own_im[:, None]
        pair_imag_part = pair_vis_re[None] * own_im[:, None] - pair_vis_im[None] * own_re[:, None]
        pair_shape = (local * local,) + pair_real_part.shape[2:]
        real_part = pair_real_part.reshape(pair_shape)
        imag_part = pair_imag_part.reshape(pair_shape)
        potentials_real_part = real_part
        potentials_imag_part = imag_part
        potentials_real_part, potentials_imag_part = transform(
            potentials_real_part, potentials_imag_part, 3, False
        )
        potentials_real_part, potentials_imag_part = transform(
            potentials_real_part, potentials_imag_part, 2, False
        )
        stacked = jnp.stack([potentials_real_part, potentials_imag_part], axis=1)
        block = lax.all_to_all(stacked, "grid", split_axis=3, concat_axis=2, tiled=True)
        pencil_real_part, pencil_imag_part = transform(block[:, 0], block[:, 1], 1, False)
        pencil_real_part = pencil_real_part * kernel[None]
        pencil_imag_part = pencil_imag_part * kernel[None]
        pencil_real_part, pencil_imag_part = transform(pencil_real_part, pencil_imag_part, 1, True)
        back = jnp.stack([pencil_real_part, pencil_imag_part], axis=1)
        result = lax.all_to_all(back, "grid", split_axis=2, concat_axis=3, tiled=True)
        potentials_real_part, potentials_imag_part = transform(result[:, 0], result[:, 1], 2, True)
        pot_re, pot_im = transform(potentials_real_part, potentials_imag_part, 3, True)
        accumulate_pot_re = pot_re
        accumulate_pot_im = pot_im
        vis_re = visitors[:, 0][None]
        vis_im = visitors[:, 1][None]
        shape = (local, local) + accumulate_pot_re.shape[1:]
        accumulate_pot_re = accumulate_pot_re.reshape(shape)
        accumulate_pot_im = accumulate_pot_im.reshape(shape)
        add_re = jnp.sum(accumulate_pot_re * vis_re - accumulate_pot_im * vis_im, axis=1)
        add_im = jnp.sum(accumulate_pot_re * vis_im + accumulate_pot_im * vis_re, axis=1)
        totals = (totals[0] + add_re, totals[1] + add_im)
    return -0.25 * jnp.stack([totals[0], totals[1]], axis=1)


def solution(mesh):
    in_specs = (P("band", None, "grid", None, None), P(None, "grid", None))
    out_specs = P("band", None, "grid", None, None)
    return jax.shard_map(body, mesh=mesh, in_specs=in_specs, out_specs=out_specs, check_vma=False)
```

profile of v0, /device:TPU:24, one launch (start us, length us, event | category | flops | bytes accessed | tf_op | source)
XLA Modules:
  0.0 190.1 jit_solution(902207428888958431)
XLA Ops:
  1.5 1.6 collective-permute-start.6
  7.9 18.3 %collective-permute-done.2 = f32[1,2,8,128,128]{4,3,1,2,0:T(8,128)S(1)} collective-permute-done((f32[1,2,8,128,128]{4,3,1,2,0:T(8,128)S(1)}, f32[1,2,8,128,128]{4,3,1,2,0:T(8,128)S(1)}, u32[]{:S(2)}, u32[]{:S(2)}) %collective-permute-start.2) | collective-permute-done | bytes 1048608 | tf_op jit(solution)/shard_map/ppermute | solution.py:23
  30.4 11.6 %collective-permute-done.9 = f32[1,2,8,128,128]{4,3,1,2,0:T(8,128)S(1)} collective-permute-done((f32[1,2,8,128,128]{4,3,1,2,0:T(8,128)}, f32[1,2,8,128,128]{4,3,1,2,0:T(8,128)S(1)}, u32[]{:S(2)}, u32[]{:S(2)}) %collective-permute-start.9) | collective-permute-done | bytes 1048608 | tf_op jit(solution)/shard_map/ppermute | solution.py:23
  42.0 1.6 collective-permute-start.7
  44.7 2.3 %collective-permute-start.12 = (f32[1,2,8,128,128]{4,3,1,2,0:T(8,128)}, f32[1,2,8,128,128]{4,3,1,2,0:T(8,128)}, u32[]{:S(2)}, u32[]{:S(2)}) collective-permute-start(f32[1,2,8,128,128]{4,3,1,2,0:T(8,128)} %add.131), channel_id=1, source_target_pairs={{96,80},{224,208},{97,81},{225,209},{98,82},{226,210},{99,83},{227... | collective-permute-start | bytes 3145736 | tf_op jit(solution)/shard_map/ppermute | solution.py:23
  47.0 1.7 collective-permute-start.11
  48.6 2.3 %collective-permute-start.10 = (f32[1,2,8,128,128]{4,3,1,2,0:T(8,128)}, f32[1,2,8,128,128]{4,3,1,2,0:T(8,128)}, u32[]{:S(2)}, u32[]{:S(2)}) collective-permute-start(f32[1,2,8,128,128]{4,3,1,2,0:T(8,128)} %add.131), channel_id=1, source_target_pairs={{32,48},{96,112},{160,176},{224,240},{33,49},{97,113},{161,177},{2... | collective-permute-start | bytes 3145736 | tf_op jit(solution)/shard_map/ppermute | solution.py:23
  54.5 14.6 %all-to-all-start = ((f32[1,2,8,128,128]{4,2,1,0,3:T(8,128)}), f32[1,2,8,128,128]{4,2,1,0,3:T(8,128)}, u32[]{:S(2)}, u32[]{:S(2)}) async-start(f32[1,2,8,128,128]{4,2,1,0,3:T(8,128)} %copy.35), calls=%async_computation | async-start | bytes 2097152 | tf_op jit(solution)/shard_map/all_to_all | solution.py:89
  69.2 3.4 %add_add_fusion = f32[1,2,8,128,128]{4,3,1,2,0:T(8,128)S(1)} fusion(f32[1,2,8,128,128]{4,3,1,2,0:T(8,128)} %collective-permute-done.6, f32[1,2,8,128,128]{4,3,1,2,0:T(8,128)} %collective-permute-done.12, f32[1,2,8,128,128]{4,3,1,2,0:T(8,128)} %collective-permute-done.11, f32[1,2,8,128,128]{4,3,1,2,0:T(8,128)} %collective-permute-done.10, ...), kind=kLoop, calls=%fused_computation.35 | loop fusion | flops 1310720 | bytes 7340032 | tf_op jit(solution)/shard_map/add | solution.py:43
  74.0 1.6 copy.50
  75.6 21.8 %all-to-all-done = f32[1,2,8,128,128]{4,2,1,0,3:T(8,128)} async-done(((f32[1,2,8,128,128]{4,2,1,0,3:T(8,128)}), f32[1,2,8,128,128]{4,2,1,0,3:T(8,128)}, u32[]{:S(2)}, u32[]{:S(2)}) %all-to-all-start) | async-done | bytes 1048608 | tf_op jit(solution)/shard_map/all_to_all | solution.py:89
  97.4 4.3 %all-to-all-start.2 = ((f32[1,2,8,128,128]{4,2,1,0,3:T(8,128)}), f32[1,2,8,128,128]{4,2,1,0,3:T(8,128)}, u32[]{:S(2)}, u32[]{:S(2)}) async-start(f32[1,2,8,128,128]{4,2,1,0,3:T(8,128)} %copy.50), calls=%async_computation.2 | async-start | bytes 2097152 | tf_op jit(solution)/shard_map/all_to_all | solution.py:89
  102.4 2.8 %convolution_bitcast_fusion.10 = f32[1,2,128,8,128]{4,2,3,1,0:T(8,128)} fusion(f32[1,2,8,16,8,128]{5,2,1,4,3,0:T(8,128)} %bitcast.23, f32[1,128,2,128]{1,3,0,2:T(8,128)S(1)} %get-tuple-element.26, f32[1,128,2,128]{1,3,0,2:T(8,128)S(1)} %get-tuple-element.29), kind=kOutput, calls=%fused_computation.10 | convolution fusion | flops 402718720 | bytes 2359296 | tf_op jit(solution)/shard_map/prnbc,rntk->ptkbc/dot_general | solution.py:58
  105.2 23.9 %all-to-all-done.2 = f32[1,2,8,128,128]{4,2,1,0,3:T(8,128)} async-done(((f32[1,2,8,128,128]{4,2,1,0,3:T(8,128)}), f32[1,2,8,128,128]{4,2,1,0,3:T(8,128)}, u32[]{:S(2)}, u32[]{:S(2)}) %all-to-all-start.2) | async-done | bytes 1048608 | tf_op jit(solution)/shard_map/all_to_all | solution.py:89
  129.1 2.0 %convolution_bitcast_fusion.5 = f32[1,2,128,8,128]{4,2,3,1,0:T(8,128)S(1)} fusion(f32[1,2,8,16,8,128]{5,2,1,4,3,0:T(8,128)} %bitcast.68, f32[1,128,2,128]{1,3,0,2:T(8,128)S(1)} %get-tuple-element.26, f32[1,128,2,128]{1,3,0,2:T(8,128)S(1)} %get-tuple-element.29), kind=kOutput, calls=%fused_computation.5 | convolution fusion | flops 402718720 | bytes 2359296 | tf_op jit(solution)/shard_map/prnbc,rntk->ptkbc/dot_general | solution.py:58
  133.0 1.6 copy.54
  134.6 3.8 %all-to-all-start.3 = ((f32[1,2,128,8,128]{4,3,1,0,2:T(8,128)}), f32[1,2,128,8,128]{4,3,1,0,2:T(8,128)S(1)}, u32[]{:S(2)}, u32[]{:S(2)}) async-start(f32[1,2,128,8,128]{4,3,1,0,2:T(8,128)} %copy.54), calls=%async_computation.3 | async-start | bytes 2097152 | tf_op jit(solution)/shard_map/all_to_all | solution.py:95
  138.5 1.8 convolution_bitcast_fusion.9
  140.3 1.6 copy.40
  141.9 21.2 %all-to-all-done.3 = f32[1,2,128,8,128]{4,3,1,0,2:T(8,128)S(1)} async-done(((f32[1,2,128,8,128]{4,3,1,0,2:T(8,128)}), f32[1,2,128,8,128]{4,3,1,0,2:T(8,128)S(1)}, u32[]{:S(2)}, u32[]{:S(2)}) %all-to-all-start.3) | async-done | bytes 1048608 | tf_op jit(solution)/shard_map/all_to_all | solution.py:95
  163.1 4.3 %all-to-all-start.1 = ((f32[1,2,128,8,128]{4,3,1,0,2:T(8,128)}), f32[1,2,128,8,128]{4,3,1,0,2:T(8,128)}, u32[]{:S(2)}, u32[]{:S(2)}) async-start(f32[1,2,128,8,128]{4,3,1,0,2:T(8,128)} %copy.40), calls=%async_computation.1 | async-start | bytes 2097152 | tf_op jit(solution)/shard_map/all_to_all | solution.py:95
  167.4 1.6 convolution_bitcast_fusion.3
  169.0 16.3 %all-to-all-done.1 = f32[1,2,128,8,128]{4,3,1,0,2:T(8,128)} async-done(((f32[1,2,128,8,128]{4,3,1,0,2:T(8,128)}), f32[1,2,128,8,128]{4,3,1,0,2:T(8,128)}, u32[]{:S(2)}, u32[]{:S(2)}) %all-to-all-start.1) | async-done | bytes 1048608 | tf_op jit(solution)/shard_map/all_to_all | solution.py:95
  185.4 1.9 %convolution_bitcast_fusion.8 = f32[2,8,128,128,1]{3,2,1,0,4:T(8,128)S(1)} fusion(f32[1,2,16,8,8,128]{5,4,1,3,2,0:T(8,128)} %bitcast.39, f32[2,128,2,128,1]{1,3,2,0,4:T(8,128)S(1)} %get-tuple-element.24), kind=kOutput, calls=%fused_computation.8 | convolution fusion | flops 402653184 | bytes 2359296 | tf_op jit(solution)/shard_map/pranc,rntk->ptakc/dot_general | solution.py:58
  (51 shorter events, 21.9 us)
Async XLA Ops:
  1.5 3.7 %collective-permute-start.6 = (f32[1,2,8,128,128]{4,3,1,2,0:T(8,128)S(1)}, f32[1,2,8,128,128]{4,3,1,2,0:T(8,128)}, u32[]{:S(2)}, u32[]{:S(2)}) collective-permute-start(f32[1,2,8,128,128]{4,3,1,2,0:T(8,128)S(1)} %get-tuple-element.20), channel_id=1, source_target_pairs={{0,128},{128,0},{1,129},{129,1},{2,130},{130,2},{3,131},{131,3},{4... | collective-permute-start | bytes 3145736 | tf_op jit(solution)/shard_map/ppermute | solution.py:42
  3.1 4.8 %collective-permute-start.1 = (f32[1,2,8,128,128]{4,3,1,2,0:T(8,128)S(1)}, f32[1,2,8,128,128]{4,3,1,2,0:T(8,128)S(1)}, u32[]{:S(2)}, u32[]{:S(2)}) collective-permute-start(f32[1,2,8,128,128]{4,3,1,2,0:T(8,128)S(1)} %get-tuple-element.19), channel_id=1, source_target_pairs={{0,32},{128,160},{1,33},{129,161},{2,34},{130,162},{3,35},{131,163... | collective-permute-start | bytes 3145736 | tf_op jit(solution)/shard_map/ppermute | solution.py:23
  3.8 22.4 %collective-permute-start.2 = (f32[1,2,8,128,128]{4,3,1,2,0:T(8,128)S(1)}, f32[1,2,8,128,128]{4,3,1,2,0:T(8,128)S(1)}, u32[]{:S(2)}, u32[]{:S(2)}) collective-permute-start(f32[1,2,8,128,128]{4,3,1,2,0:T(8,128)S(1)} %get-tuple-element.19), channel_id=1, source_target_pairs={{0,96},{128,224},{1,97},{129,225},{2,98},{130,226},{3,99},{131,227... | collective-permute-start | bytes 3145736 | tf_op jit(solution)/shard_map/ppermute | solution.py:23
  5.1 23.3 %collective-permute-start.8 = (f32[1,2,8,128,128]{4,3,1,2,0:T(8,128)}, f32[1,2,8,128,128]{4,3,1,2,0:T(8,128)S(1)}, u32[]{:S(2)}, u32[]{:S(2)}) collective-permute-start(f32[1,2,8,128,128]{4,3,1,2,0:T(8,128)} %collective-permute-done.6), channel_id=1, source_target_pairs={{0,32},{128,160},{1,33},{129,161},{2,34},{130,162},{3,35},{131,163... | collective-permute-start | bytes 3145736 | tf_op jit(solution)/shard_map/ppermute | solution.py:23
  5.9 36.1 %collective-permute-start.9 = (f32[1,2,8,128,128]{4,3,1,2,0:T(8,128)}, f32[1,2,8,128,128]{4,3,1,2,0:T(8,128)S(1)}, u32[]{:S(2)}, u32[]{:S(2)}) collective-permute-start(f32[1,2,8,128,128]{4,3,1,2,0:T(8,128)} %collective-permute-done.6), channel_id=1, source_target_pairs={{0,96},{128,224},{1,97},{129,225},{2,98},{130,226},{3,99},{131,227... | collective-permute-start | bytes 3145736 | tf_op jit(solution)/shard_map/ppermute | solution.py:23
  7.2 37.5 %collective-permute-start = (f32[1,2,8,128,128]{4,3,1,2,0:T(8,128)S(1)}, f32[1,2,8,128,128]{4,3,1,2,0:T(8,128)S(1)}, u32[]{:S(2)}, u32[]{:S(2)}) collective-permute-start(f32[1,2,8,128,128]{4,3,1,2,0:T(8,128)S(1)} %get-tuple-element.19), channel_id=1, source_target_pairs={{0,16},{128,144},{1,17},{129,145},{2,18},{130,146},{3,19},{131,147... | collective-permute-start | bytes 3145736 | tf_op jit(solution)/shard_map/ppermute | solution.py:23
  26.3 20.6 %collective-permute-start.5 = (f32[1,2,8,128,128]{4,3,1,2,0:T(8,128)S(1)}, f32[1,2,8,128,128]{4,3,1,2,0:T(8,128)S(1)}, u32[]{:S(2)}, u32[]{:S(2)}) collective-permute-start(f32[1,2,8,128,128]{4,3,1,2,0:T(8,128)S(1)} %add.124), channel_id=1, source_target_pairs={{96,80},{224,208},{97,81},{225,209},{98,82},{226,210},{99,83},{227... | collective-permute-start | bytes 3145736 | tf_op jit(solution)/shard_map/ppermute | solution.py:23
  27.7 20.9 %collective-permute-start.4 = (f32[1,2,8,128,128]{4,3,1,2,0:T(8,128)S(1)}, f32[1,2,8,128,128]{4,3,1,2,0:T(8,128)S(1)}, u32[]{:S(2)}, u32[]{:S(2)}) collective-permute-start(f32[1,2,8,128,128]{4,3,1,2,0:T(8,128)S(1)} %add.124), channel_id=1, source_target_pairs={{32,64},{160,192},{33,65},{161,193},{34,66},{162,194},{35,67},{163... | collective-permute-start | bytes 3145736 | tf_op jit(solution)/shard_map/ppermute | solution.py:23
  28.5 22.5 %collective-permute-start.3 = (f32[1,2,8,128,128]{4,3,1,2,0:T(8,128)S(1)}, f32[1,2,8,128,128]{4,3,1,2,0:T(8,128)S(1)}, u32[]{:S(2)}, u32[]{:S(2)}) collective-permute-start(f32[1,2,8,128,128]{4,3,1,2,0:T(8,128)S(1)} %add.124), channel_id=1, source_target_pairs={{32,48},{96,112},{160,176},{224,240},{33,49},{97,113},{161,177},{2... | collective-permute-start | bytes 3145736 | tf_op jit(solution)/shard_map/ppermute | solution.py:23
  42.0 27.1 %collective-permute-start.7 = (f32[1,2,8,128,128]{4,3,1,2,0:T(8,128)}, f32[1,2,8,128,128]{4,3,1,2,0:T(8,128)}, u32[]{:S(2)}, u32[]{:S(2)}) collective-permute-start(f32[1,2,8,128,128]{4,3,1,2,0:T(8,128)} %collective-permute-done.6), channel_id=1, source_target_pairs={{0,16},{128,144},{1,17},{129,145},{2,18},{130,146},{3,19},{131,147... | collective-permute-start | bytes 3145736 | tf_op jit(solution)/shard_map/ppermute | solution.py:23
  44.7 24.4 %collective-permute-start.12 = (f32[1,2,8,128,128]{4,3,1,2,0:T(8,128)}, f32[1,2,8,128,128]{4,3,1,2,0:T(8,128)}, u32[]{:S(2)}, u32[]{:S(2)}) collective-permute-start(f32[1,2,8,128,128]{4,3,1,2,0:T(8,128)} %add.131), channel_id=1, source_target_pairs={{96,80},{224,208},{97,81},{225,209},{98,82},{226,210},{99,83},{227... | collective-permute-start | bytes 3145736 | tf_op jit(solution)/shard_map/ppermute | solution.py:23
  47.0 22.2 %collective-permute-start.11 = (f32[1,2,8,128,128]{4,3,1,2,0:T(8,128)}, f32[1,2,8,128,128]{4,3,1,2,0:T(8,128)}, u32[]{:S(2)}, u32[]{:S(2)}) collective-permute-start(f32[1,2,8,128,128]{4,3,1,2,0:T(8,128)} %add.131), channel_id=1, source_target_pairs={{32,64},{160,192},{33,65},{161,193},{34,66},{162,194},{35,67},{163... | collective-permute-start | bytes 3145736 | tf_op jit(solution)/shard_map/ppermute | solution.py:23
  48.6 20.5 %collective-permute-start.10 = (f32[1,2,8,128,128]{4,3,1,2,0:T(8,128)}, f32[1,2,8,128,128]{4,3,1,2,0:T(8,128)}, u32[]{:S(2)}, u32[]{:S(2)}) collective-permute-start(f32[1,2,8,128,128]{4,3,1,2,0:T(8,128)} %add.131), channel_id=1, source_target_pairs={{32,48},{96,112},{160,176},{224,240},{33,49},{97,113},{161,177},{2... | collective-permute-start | bytes 3145736 | tf_op jit(solution)/shard_map/ppermute | solution.py:23
  54.5 42.9 %all-to-all-start = ((f32[1,2,8,128,128]{4,2,1,0,3:T(8,128)}), f32[1,2,8,128,128]{4,2,1,0,3:T(8,128)}, u32[]{:S(2)}, u32[]{:S(2)}) async-start(f32[1,2,8,128,128]{4,2,1,0,3:T(8,128)} %copy.35), calls=%async_computation | async-start | bytes 2097152 | tf_op jit(solution)/shard_map/all_to_all | solution.py:89
  69.1 3.5 %copy-start = (f32[1,2,8,128,128]{4,3,2,1,0:T(8,128)S(1)}, f32[1,2,8,128,128]{4,3,2,1,0:T(8,128)}, u32[]{:S(2)}) copy-start(f32[1,2,8,128,128]{4,3,2,1,0:T(8,128)} %param.2) | copy-start | bytes 3145732
  97.4 31.8 %all-to-all-start.2 = ((f32[1,2,8,128,128]{4,2,1,0,3:T(8,128)}), f32[1,2,8,128,128]{4,2,1,0,3:T(8,128)}, u32[]{:S(2)}, u32[]{:S(2)}) async-start(f32[1,2,8,128,128]{4,2,1,0,3:T(8,128)} %copy.50), calls=%async_computation.2 | async-start | bytes 2097152 | tf_op jit(solution)/shard_map/all_to_all | solution.py:89
  129.1 2.0 %copy-start.2 = (f32[1,2,128,8,128]{4,2,3,1,0:T(8,128)S(1)}, f32[1,2,128,8,128]{4,2,3,1,0:T(8,128)}, u32[]{:S(2)}) copy-start(f32[1,2,128,8,128]{4,2,3,1,0:T(8,128)} %convolution_bitcast_fusion.10) | copy-start | bytes 3145732
  129.1 2.0 %copy-start.4 = (f32[128,8,128]{2,1,0:T(8,128)S(1)}, f32[128,8,128]{2,1,0:T(8,128)}, u32[]{:S(2)}) copy-start(f32[128,8,128]{2,1,0:T(8,128)} %param.3) | copy-start | bytes 1572868
  134.6 28.5 %all-to-all-start.3 = ((f32[1,2,128,8,128]{4,3,1,0,2:T(8,128)}), f32[1,2,128,8,128]{4,3,1,0,2:T(8,128)S(1)}, u32[]{:S(2)}, u32[]{:S(2)}) async-start(f32[1,2,128,8,128]{4,3,1,0,2:T(8,128)} %copy.54), calls=%async_computation.3 | async-start | bytes 2097152 | tf_op jit(solution)/shard_map/all_to_all | solution.py:95
  163.1 22.3 %all-to-all-start.1 = ((f32[1,2,128,8,128]{4,3,1,0,2:T(8,128)}), f32[1,2,128,8,128]{4,3,1,0,2:T(8,128)}, u32[]{:S(2)}, u32[]{:S(2)}) async-start(f32[1,2,128,8,128]{4,3,1,0,2:T(8,128)} %copy.40), calls=%async_computation.1 | async-start | bytes 2097152 | tf_op jit(solution)/shard_map/all_to_all | solution.py:95
  185.4 2.0 %copy-start.1 = (f32[2,8,128,128,1]{3,2,1,0,4:T(8,128)S(1)}, f32[2,8,128,128,1]{3,2,1,0,4:T(8,128)}, u32[]{:S(2)}) copy-start(f32[2,8,128,128,1]{3,2,1,0,4:T(8,128)} %convolution_bitcast_fusion.3) | copy-start | bytes 3145732
  185.4 2.0 %copy-start.3 = (f32[2,128,2,128]{1,3,2,0:T(8,128)S(1)}, f32[2,128,2,128]{1,3,2,0:T(8,128)}, u32[]{:S(2)}) copy-start(f32[2,128,2,128]{1,3,2,0:T(8,128)} %get-tuple-element.23) | copy-start | bytes 786436
where the time goes:
time: 192 us; the launch traced here: 190 us
  waiting for transfers between devices  113 us (59%)
  starting transfers between devices  44.8 us (23%)
  matrix products  14.5 us (8%)
  other arithmetic  9.97 us (5%)
  local copies, waits for them, and re-layouts  7.43 us (4%)
    all_to_all x2, waiting for transfers between devices, body(): lax.all_to_all(stacked, 'grid', split_axis=3, concat_axis=2, tiled=True)  45.7 us
    all_to_all x2, waiting for transfers between devices, body(): lax.all_to_all(back, 'grid', split_axis=2, concat_axis=3, tiled=True)  37.6 us
    ppermute x12, waiting for transfers between devices, send(): lax.ppermute(operand, axis, [(band_place(h, *a), band_place(h, *b)) for h...  29.9 us
    all_to_all x2, starting transfers between devices, body(): lax.all_to_all(stacked, 'grid', split_axis=3, concat_axis=2, tiled=True)  18.9 us
    ppermute x12, starting transfers between devices, send(): lax.ppermute(operand, axis, [(band_place(h, *a), band_place(h, *b)) for h...  16 us
    dot_general x12, matrix products, transform(): jnp.einsum(fused_forms[axis_dim], values, table, precision=lax.Precision....  14.5 us
    all_to_all x2, starting transfers between devices, body(): lax.all_to_all(back, 'grid', split_axis=2, concat_axis=3, tiled=True)  8.17 us
    transpose x4, local copies, waits for them, and re-layouts, transform(): jnp.einsum(fused_forms[axis_dim], values, table, precision=lax.Precision....  6.34 us
  transfers between devices with their start and end apart: 17, of which 6 were waited for; matrix products, arithmetic and copies ran while one was open for 11% of the time, Pallas kernels for 0%

commit v1 on v0

--- a/solution.py
+++ b/solution.py
@@ -65,16 +65,13 @@
     own_re = bands[:, 0]
     own_im = bands[:, 1]
     totals = (jnp.zeros_like(own_re), jnp.zeros_like(own_im))
-    for visit_index, visitors in enumerate(visitors_of(bands, "band")):
-        if visit_index:
-            own, visitors = lax.optimization_barrier((bands, visitors))
-            own_re = own[:, 0]
-            own_im = own[:, 1]
+    for visitors in [jnp.concatenate(visitors_of(bands, "band"), axis=0)]:
+        count = visitors.shape[0]
         pair_vis_re = visitors[:, 0]
         pair_vis_im = visitors[:, 1]
         pair_real_part = pair_vis_re[None] * own_re[:, None] + pair_vis_im[None] * own_im[:, None]
         pair_imag_part = pair_vis_re[None] * own_im[:, None] - pair_vis_im[None] * own_re[:, None]
-        pair_shape = (local * local,) + pair_real_part.shape[2:]
+        pair_shape = (local * count,) + pair_real_part.shape[2:]
         real_part = pair_real_part.reshape(pair_shape)
         imag_part = pair_imag_part.reshape(pair_shape)
         potentials_real_part = real_part
@@ -99,7 +96,7 @@
         accumulate_pot_im = pot_im
         vis_re = visitors[:, 0][None]
         vis_im = visitors[:, 1][None]
-        shape = (local, local) + accumulate_pot_re.shape[1:]
+        shape = (local, count) + accumulate_pot_re.shape[1:]
         accumulate_pot_re = accumulate_pot_re.reshape(shape)
         accumulate_pot_im = accumulate_pot_im.reshape(shape)
         add_re = jnp.sum(accumulate_pot_re * vis_re - accumulate_pot_im * vis_im, axis=1)

time: 192 us -> 199 us (1.036)
  the two profiles are of different devices: /device:TPU:24 before, /device:TPU:16 now
where the time goes in v1:
time: 199 us; the launch traced here: 198 us
  waiting for transfers between devices  99.5 us (50%)
  blocking collectives  53.7 us (27%)
  starting transfers between devices  25.4 us (13%)
  matrix products  8.71 us (4%)
  local copies, waits for them, and re-layouts  5.64 us (3%)
  other arithmetic  4.83 us (2%)
    all_to_all x1, waiting for transfers between devices, body(): lax.all_to_all(stacked, 'grid', split_axis=3, concat_axis=2, tiled=True)  55.4 us
    all_to_all x1, blocking collectives, body(): lax.all_to_all(back, 'grid', split_axis=2, concat_axis=3, tiled=True)  53.7 us
    ppermute x12, waiting for transfers between devices, send(): lax.ppermute(operand, axis, [(band_place(h, *a), band_place(h, *b)) for h...  44.1 us
    all_to_all x1, starting transfers between devices, body(): lax.all_to_all(stacked, 'grid', split_axis=3, concat_axis=2, tiled=True)  14.7 us
    ppermute x12, starting transfers between devices, send(): lax.ppermute(operand, axis, [(band_place(h, *a), band_place(h, *b)) for h...  9.98 us
    dot_general x6, matrix products, transform(): jnp.einsum(fused_forms[axis_dim], values, table, precision=lax.Precision....  8.71 us
  transfers between devices with their start and end apart: 14, of which 3 were waited for; matrix products, arithmetic and copies ran while one was open for 1% of the time, Pallas kernels for 0%

profile of v1, /device:TPU:16, one launch (start us, length us, event | category | flops | bytes accessed | tf_op | source)
XLA Modules:
  0.0 198.2 jit_solution(9371771761826557927)
XLA Ops:
  0.0 1.5 broadcast_select_fusion
  2.2 0.7 collective-permute-start.1
  2.9 0.7 collective-permute-start.2
  3.7 0.7 collective-permute-start.8
  5.2 0.7 collective-permute-start
  6.1 0.9 collective-permute-start.3
  7.0 1.3 collective-permute-start.4
  8.3 0.7 collective-permute-start.5
  9.0 0.7 collective-permute-start.7
  10.6 1.3 collective-permute-start.11
  11.9 29.3 %collective-permute-done.4 = f32[1,2,8,128,128]{4,3,1,2,0:T(8,128)S(1)} collective-permute-done((f32[1,2,8,128,128]{4,3,1,2,0:T(8,128)S(1)}, f32[1,2,8,128,128]{4,3,1,2,0:T(8,128)S(1)}, u32[]{:S(2)}, u32[]{:S(2)}) %collective-permute-start.4) | collective-permute-done | bytes 1048608 | tf_op jit(solution)/shard_map/ppermute | solution.py:23
  43.3 14.8 %collective-permute-done.11 = f32[1,2,8,128,128]{4,3,1,2,0:T(8,128)S(1)} collective-permute-done((f32[1,2,8,128,128]{4,3,1,2,0:T(8,128)S(1)}, f32[1,2,8,128,128]{4,3,1,2,0:T(8,128)S(1)}, u32[]{:S(2)}, u32[]{:S(2)}) %collective-permute-start.11) | collective-permute-done | bytes 1048608 | tf_op jit(solution)/shard_map/ppermute | solution.py:23
  59.1 1.2 fusion.2
  60.3 1.2 fusion.19
  61.5 2.5 %copy.45 = f32[2,2,8,128,128]{4,2,0,1,3:T(8,128)} copy(f32[2,2,8,128,128]{4,3,2,0,1:T(8,128)S(1)} %fusion.19) | data formatting | bytes 4194304 | tf_op jit(solution)/shard_map/pranc,rntk->ptakc/transpose | solution.py:58
  64.1 14.7 %all-to-all-start = ((f32[2,2,8,128,128]{4,2,0,1,3:T(8,128)}), f32[2,2,8,128,128]{4,2,0,1,3:T(8,128)}, u32[]{:S(2)}, u32[]{:S(2)}) async-start(f32[2,2,8,128,128]{4,2,0,1,3:T(8,128)} %copy.45), calls=%async_computation | async-start | bytes 4194304 | tf_op jit(solution)/shard_map/all_to_all | solution.py:86
  79.0 55.4 %all-to-all-done = f32[2,2,8,128,128]{4,2,0,1,3:T(8,128)} async-done(((f32[2,2,8,128,128]{4,2,0,1,3:T(8,128)}), f32[2,2,8,128,128]{4,2,0,1,3:T(8,128)}, u32[]{:S(2)}, u32[]{:S(2)}) %all-to-all-start) | async-done | bytes 2097184 | tf_op jit(solution)/shard_map/all_to_all | solution.py:86
  134.4 2.8 %fusion.22 = f32[2,2,128,8,128]{4,2,3,0,1:T(8,128)S(1)} fusion(f32[2,2,8,16,8,128]{5,2,0,1,4,3:T(8,128)} %bitcast.23, f32[1,128,2,128]{1,3,0,2:T(8,128)S(1)} %get-tuple-element.17, f32[1,128,2,128]{1,3,0,2:T(8,128)S(1)} %get-tuple-element.20), kind=kOutput, calls=%fused_computation.23 | convolution fusion | flops 805371904 | bytes 4456448 | tf_op jit(solution)/shard_map/prnbc,rntk->ptkbc/dot_general | solution.py:58
  137.4 1.2 fusion.16
  138.7 1.2 copy.50
  139.9 53.7 %all_to_all.36 = f32[2,2,128,8,128]{4,3,0,1,2:T(8,128)S(1)} all-to-all(f32[2,2,128,8,128]{4,3,0,1,2:T(8,128)S(1)} %copy.50), channel_id=1, replica_groups=mesh['band'=16,'grid'=16] {'grid'}, dimensions={2} | all-to-all | bytes 4194304 | tf_op jit(solution)/shard_map/all_to_all | solution.py:92
  193.6 1.3 fusion.5
  194.9 1.1 fusion.25
  196.9 1.3 copy.59
  (36 shorter events, 6.9 us)
Async XLA Ops:
  1.5 2.2 %collective-permute-start.6 = (f32[1,2,8,128,128]{4,3,1,2,0:T(8,128)S(1)}, f32[1,2,8,128,128]{4,3,1,2,0:T(8,128)S(1)}, u32[]{:S(2)}, u32[]{:S(2)}) collective-permute-start(f32[1,2,8,128,128]{4,3,1,2,0:T(8,128)S(1)} %get-tuple-element.13), channel_id=1, source_target_pairs={{0,128},{128,0},{1,129},{129,1},{2,130},{130,2},{3,131},{131,3},{4... | collective-permute-start | bytes 3145736 | tf_op jit(solution)/shard_map/ppermute | solution.py:42
  2.2 3.7 %collective-permute-start.1 = (f32[1,2,8,128,128]{4,3,1,2,0:T(8,128)S(1)}, f32[1,2,8,128,128]{4,3,1,2,0:T(8,128)S(1)}, u32[]{:S(2)}, u32[]{:S(2)}) collective-permute-start(f32[1,2,8,128,128]{4,3,1,2,0:T(8,128)S(1)} %get-tuple-element.12), channel_id=1, source_target_pairs={{0,32},{128,160},{1,33},{129,161},{2,34},{130,162},{3,35},{131,163... | collective-permute-start | bytes 3145736 | tf_op jit(solution)/shard_map/ppermute | solution.py:23
  2.9 3.0 %collective-permute-start.2 = (f32[1,2,8,128,128]{4,3,1,2,0:T(8,128)S(1)}, f32[1,2,8,128,128]{4,3,1,2,0:T(8,128)S(1)}, u32[]{:S(2)}, u32[]{:S(2)}) collective-permute-start(f32[1,2,8,128,128]{4,3,1,2,0:T(8,128)S(1)} %get-tuple-element.12), channel_id=1, source_target_pairs={{0,96},{128,224},{1,97},{129,225},{2,98},{130,226},{3,99},{131,227... | collective-permute-start | bytes 3145736 | tf_op jit(solution)/shard_map/ppermute | solution.py:23
  3.7 4.6 %collective-permute-start.8 = (f32[1,2,8,128,128]{4,3,1,2,0:T(8,128)S(1)}, f32[1,2,8,128,128]{4,3,1,2,0:T(8,128)S(1)}, u32[]{:S(2)}, u32[]{:S(2)}) collective-permute-start(f32[1,2,8,128,128]{4,3,1,2,0:T(8,128)S(1)} %collective-permute-done.6), channel_id=1, source_target_pairs={{0,32},{128,160},{1,33},{129,161},{2,34},{130,162},{3,35},{131,163... | collective-permute-start | bytes 3145736 | tf_op jit(solution)/shard_map/ppermute | solution.py:23
  4.4 4.6 %collective-permute-start.9 = (f32[1,2,8,128,128]{4,3,1,2,0:T(8,128)S(1)}, f32[1,2,8,128,128]{4,3,1,2,0:T(8,128)S(1)}, u32[]{:S(2)}, u32[]{:S(2)}) collective-permute-start(f32[1,2,8,128,128]{4,3,1,2,0:T(8,128)S(1)} %collective-permute-done.6), channel_id=1, source_target_pairs={{0,96},{128,224},{1,97},{129,225},{2,98},{130,226},{3,99},{131,227... | collective-permute-start | bytes 3145736 | tf_op jit(solution)/shard_map/ppermute | solution.py:23
  5.2 4.7 %collective-permute-start = (f32[1,2,8,128,128]{4,3,1,2,0:T(8,128)S(1)}, f32[1,2,8,128,128]{4,3,1,2,0:T(8,128)S(1)}, u32[]{:S(2)}, u32[]{:S(2)}) collective-permute-start(f32[1,2,8,128,128]{4,3,1,2,0:T(8,128)S(1)} %get-tuple-element.12), channel_id=1, source_target_pairs={{0,16},{128,144},{1,17},{129,145},{2,18},{130,146},{3,19},{131,147... | collective-permute-start | bytes 3145736 | tf_op jit(solution)/shard_map/ppermute | solution.py:23
  6.1 36.5 %copy-start = (f32[1,2,8,128,128]{4,3,2,1,0:T(8,128)S(1)}, f32[1,2,8,128,128]{4,3,2,1,0:T(8,128)}, u32[]{:S(2)}) copy-start(f32[1,2,8,128,128]{4,3,2,1,0:T(8,128)} %param.2) | copy-start | bytes 3145732
  6.1 4.6 %collective-permute-start.3 = (f32[1,2,8,128,128]{4,3,1,2,0:T(8,128)S(1)}, f32[1,2,8,128,128]{4,3,1,2,0:T(8,128)S(1)}, u32[]{:S(2)}, u32[]{:S(2)}) collective-permute-start(f32[1,2,8,128,128]{4,3,1,2,0:T(8,128)S(1)} %add.106), channel_id=1, source_target_pairs={{32,48},{96,112},{160,176},{224,240},{33,49},{97,113},{161,177},{2... | collective-permute-start | bytes 3145736 | tf_op jit(solution)/shard_map/ppermute | solution.py:23
  7.0 34.3 %collective-permute-start.4 = (f32[1,2,8,128,128]{4,3,1,2,0:T(8,128)S(1)}, f32[1,2,8,128,128]{4,3,1,2,0:T(8,128)S(1)}, u32[]{:S(2)}, u32[]{:S(2)}) collective-permute-start(f32[1,2,8,128,128]{4,3,1,2,0:T(8,128)S(1)} %add.106), channel_id=1, source_target_pairs={{32,64},{160,192},{33,65},{161,193},{34,66},{162,194},{35,67},{163... | collective-permute-start | bytes 3145736 | tf_op jit(solution)/shard_map/ppermute | solution.py:23
  8.3 34.4 %collective-permute-start.5 = (f32[1,2,8,128,128]{4,3,1,2,0:T(8,128)S(1)}, f32[1,2,8,128,128]{4,3,1,2,0:T(8,128)S(1)}, u32[]{:S(2)}, u32[]{:S(2)}) collective-permute-start(f32[1,2,8,128,128]{4,3,1,2,0:T(8,128)S(1)} %add.106), channel_id=1, source_target_pairs={{96,80},{224,208},{97,81},{225,209},{98,82},{226,210},{99,83},{227... | collective-permute-start | bytes 3145736 | tf_op jit(solution)/shard_map/ppermute | solution.py:23
  9.0 34.2 %collective-permute-start.7 = (f32[1,2,8,128,128]{4,3,1,2,0:T(8,128)S(1)}, f32[1,2,8,128,128]{4,3,1,2,0:T(8,128)S(1)}, u32[]{:S(2)}, u32[]{:S(2)}) collective-permute-start(f32[1,2,8,128,128]{4,3,1,2,0:T(8,128)S(1)} %collective-permute-done.6), channel_id=1, source_target_pairs={{0,16},{128,144},{1,17},{129,145},{2,18},{130,146},{3,19},{131,147... | collective-permute-start | bytes 3145736 | tf_op jit(solution)/shard_map/ppermute | solution.py:23
  9.9 33.4 %collective-permute-start.10 = (f32[1,2,8,128,128]{4,3,1,2,0:T(8,128)S(1)}, f32[1,2,8,128,128]{4,3,1,2,0:T(8,128)S(1)}, u32[]{:S(2)}, u32[]{:S(2)}) collective-permute-start(f32[1,2,8,128,128]{4,3,1,2,0:T(8,128)S(1)} %add.112), channel_id=1, source_target_pairs={{32,48},{96,112},{160,176},{224,240},{33,49},{97,113},{161,177},{2... | collective-permute-start | bytes 3145736 | tf_op jit(solution)/shard_map/ppermute | solution.py:23
  10.6 47.4 %collective-permute-start.11 = (f32[1,2,8,128,128]{4,3,1,2,0:T(8,128)S(1)}, f32[1,2,8,128,128]{4,3,1,2,0:T(8,128)S(1)}, u32[]{:S(2)}, u32[]{:S(2)}) collective-permute-start(f32[1,2,8,128,128]{4,3,1,2,0:T(8,128)S(1)} %add.112), channel_id=1, source_target_pairs={{32,64},{160,192},{33,65},{161,193},{34,66},{162,194},{35,67},{163... | collective-permute-start | bytes 3145736 | tf_op jit(solution)/shard_map/ppermute | solution.py:23
  41.2 16.8 %collective-permute-start.12 = (f32[1,2,8,128,128]{4,3,1,2,0:T(8,128)S(1)}, f32[1,2,8,128,128]{4,3,1,2,0:T(8,128)S(1)}, u32[]{:S(2)}, u32[]{:S(2)}) collective-permute-start(f32[1,2,8,128,128]{4,3,1,2,0:T(8,128)S(1)} %add.112), channel_id=1, source_target_pairs={{96,80},{224,208},{97,81},{225,209},{98,82},{226,210},{99,83},{227... | collective-permute-start | bytes 3145736 | tf_op jit(solution)/shard_map/ppermute | solution.py:23
  64.0 14.7 %copy-start.1 = (f32[128,8,128]{2,1,0:T(8,128)S(1)}, f32[128,8,128]{2,1,0:T(8,128)}, u32[]{:S(2)}) copy-start(f32[128,8,128]{2,1,0:T(8,128)} %param.3) | copy-start | bytes 1572868
  64.1 70.4 %all-to-all-start = ((f32[2,2,8,128,128]{4,2,0,1,3:T(8,128)}), f32[2,2,8,128,128]{4,2,0,1,3:T(8,128)}, u32[]{:S(2)}, u32[]{:S(2)}) async-start(f32[2,2,8,128,128]{4,2,0,1,3:T(8,128)} %copy.45), calls=%async_computation | async-start | bytes 4194304 | tf_op jit(solution)/shard_map/all_to_all | solution.py:86

commit v2 on v0

--- a/solution.py
+++ b/solution.py
@@ -18,29 +18,35 @@
     return half * 8 + row * 2 + core
 
 
-def half_tree(value, axis):
-    def send(operand, pairs):
-        return lax.ppermute(operand, axis, [(band_place(h, *a), band_place(h, *b)) for h in (0, 1) for a, b in pairs])
-
-    first = [send(value, [((0, 0), (0, 1))]), send(value, [((0, 0), (1, 0))]), send(value, [((0, 0), (3, 0))])]
-    relay = first[1] + first[2]
-    second = [
-        send(relay, [((1, 0), (1, 1)), ((3, 0), (3, 1))]),
-        send(relay, [((1, 0), (2, 0))]),
-        send(relay, [((3, 0), (2, 1))]),
-    ]
-    total = first[0] + relay
-    for part in second:
-        total = total + part
-    return total
+def send(operand, axis, pairs):
+    return lax.ppermute(operand, axis, [(band_place(h, *a), band_place(h, *b)) for h in (0, 1) for a, b in pairs])
 
 
 def visitors_of(bands, axis):
-    index = lax.axis_index(axis)
-    head = index % 8 == 0
-    own = jnp.where(head, bands, 0).astype(bands.dtype)
-    crossed = lax.ppermute(bands, axis, [(0, 8), (8, 0)])
-    return [own + half_tree(own, axis), crossed + half_tree(crossed, axis)]
+    place = lax.axis_index(axis) % 8
+
+    def at(*places):
+        hit = place == places[0]
+        for other in places[1:]:
+            hit = hit | (place == other)
+        return hit
+
+    own_head = jnp.where(at(0), bands, 0).astype(bands.dtype)
+    crossed_head = lax.ppermute(bands, axis, [(0, 8), (8, 0)])
+    first = [send(own_head, axis, [((0, 0), pair)]) for pair in ((0, 1), (1, 0), (3, 0))]
+    relay = first[1] + first[2]
+    mixed = relay + crossed_head
+    q1 = send(mixed, axis, [((1, 0), (1, 1)), ((3, 0), (3, 1)), ((0, 0), (0, 1))])
+    q2 = send(mixed, axis, [((1, 0), (2, 0)), ((0, 0), (1, 0))])
+    q3 = send(mixed, axis, [((3, 0), (2, 1)), ((0, 0), (3, 0))])
+    zero = jnp.zeros_like(bands)
+    own = own_head + first[0] + relay + jnp.where(at(3, 7), q1, zero) + jnp.where(at(4), q2, zero)
+    own = own + jnp.where(at(5), q3, zero)
+    crossed_relay = jnp.where(at(2), q2, zero) + jnp.where(at(6), q3, zero)
+    third_a = send(crossed_relay, axis, [((1, 0), (1, 1)), ((3, 0), (2, 1))])
+    third_b = send(crossed_relay, axis, [((1, 0), (2, 0)), ((3, 0), (3, 1))])
+    crossed = crossed_head + jnp.where(at(1), q1, zero) + crossed_relay + third_a + third_b
+    return [own, crossed]
 
 
 def dft_tables(length):

time: 192 us -> 199 us (1.036)
  waiting for transfers between devices: 113 us -> 129 us
  starting transfers between devices: 44.8 us -> 33.3 us
  other arithmetic: 9.97 us -> 13.7 us
    ppermute x12 -> x8, waiting for transfers between devices: 29.9 us -> 44.5 us  [send(): lax.ppermute(operand, axis, [(band_place(h, *a), band_place(h, *b)) for h...]
    all_to_all x2, starting transfers between devices: 18.9 us -> 11.2 us  [body(): lax.all_to_all(stacked, 'grid', split_axis=3, concat_axis=2, tiled=True)]
    add x4 -> x3, other arithmetic: 5.2 us -> 8.31 us  [the longest x1 4.63 us: visitors_of(): own = own + jnp.where(at(5), q3, zero)]
    ppermute x12 -> x8, starting transfers between devices: 16 us -> 13.2 us  [send(): lax.ppermute(operand, axis, [(band_place(h, *a), band_place(h, *b)) for h...]
  transfers between devices with their start and end apart: 17 -> 13, of which waited for: 6 -> 6; matrix products, arithmetic and copies ran while one was open for 11% -> 10% of each run, Pallas kernels for 0% -> 0%
where the time goes in v2:
time: 199 us; the launch traced here: 198 us
  waiting for transfers between devices  129 us (65%)
  starting transfers between devices  33.3 us (17%)
  other arithmetic  13.7 us (7%)
  matrix products  13.2 us (7%)
  local copies, waits for them, and re-layouts  9.08 us (5%)
    all_to_all x2, waiting for transfers between devices, body(): lax.all_to_all(stacked, 'grid', split_axis=3, concat_axis=2, tiled=True)  46.9 us
    ppermute x8, waiting for transfers between devices, send(): lax.ppermute(operand, axis, [(band_place(h, *a), band_place(h, *b)) for h...  44.5 us
    all_to_all x2, waiting for transfers between devices, body(): lax.all_to_all(back, 'grid', split_axis=2, concat_axis=3, tiled=True)  37.1 us
    dot_general x12, matrix products, transform(): jnp.einsum(fused_forms[axis_dim], values, table, precision=lax.Precision....  13.2 us
    ppermute x8, starting transfers between devices, send(): lax.ppermute(operand, axis, [(band_place(h, *a), band_place(h, *b)) for h...  13.2 us
    all_to_all x2, starting transfers between devices, body(): lax.all_to_all(stacked, 'grid', split_axis=3, concat_axis=2, tiled=True)  11.2 us
    all_to_all x2, starting transfers between devices, body(): lax.all_to_all(back, 'grid', split_axis=2, concat_axis=3, tiled=True)  8.18 us
    transpose x4, local copies, waits for them, and re-layouts, transform(): jnp.einsum(fused_forms[axis_dim], values, table, precision=lax.Precision....  6.37 us
  transfers between devices with their start and end apart: 13, of which 6 were waited for; matrix products, arithmetic and copies ran while one was open for 10% of the time, Pallas kernels for 0%

profile of v2, /device:TPU:24, one launch (start us, length us, event | category | flops | bytes accessed | tf_op | source)
XLA Modules:
  0.0 198.1 jit_solution(18024951137190167481)
XLA Ops:
  0.0 2.4 %broadcast_select_fusion = (f32[1,2,8,128,128]{4,3,1,2,0:T(8,128)}, f32[1,2,8,128,128]{4,3,1,2,0:T(8,128)S(1)}) fusion(pred[]{:T(512)S(6)} %eq.39, f32[1,2,8,128,128]{4,3,2,1,0:T(8,128)} %param.2), kind=kLoop, calls=%fused_computation.57 | loop fusion | flops 262144 | bytes 3145729 | tf_op jit(solution)/shard_map/jit(_where)/select_n | solution.py:34
  5.2 1.6 collective-permute-start
  6.8 14.4 %collective-permute-done.2 = f32[1,2,8,128,128]{4,3,1,2,0:T(8,128)S(1)} collective-permute-done((f32[1,2,8,128,128]{4,3,1,2,0:T(8,128)}, f32[1,2,8,128,128]{4,3,1,2,0:T(8,128)S(1)}, u32[]{:S(2)}, u32[]{:S(2)}) %collective-permute-start.2) | collective-permute-done | bytes 1048608 | tf_op jit(solution)/shard_map/ppermute | solution.py:22
  24.0 1.7 collective-permute-start.5
  25.6 1.9 collective-permute-start.6
  29.8 30.0 %collective-permute-done.6 = f32[1,2,8,128,128]{4,3,1,2,0:T(8,128)} collective-permute-done((f32[1,2,8,128,128]{4,3,1,2,0:T(8,128)}, f32[1,2,8,128,128]{4,3,1,2,0:T(8,128)}, u32[]{:S(2)}, u32[]{:S(2)}) %collective-permute-start.6) | collective-permute-done | bytes 1048608 | tf_op jit(solution)/shard_map/ppermute | solution.py:22
  59.8 4.6 %select_add_fusion.1 = (f32[1,2,8,128,128]{4,3,1,2,0:T(8,128)S(1)}, f32[1,2,8,128,128]{4,3,1,2,0:T(8,128)}) fusion(f32[1,2,8,128,128]{4,3,1,2,0:T(8,128)} %collective-permute-done.6, f32[1,2,8,128,128]{4,3,1,2,0:T(8,128)} %collective-permute-done.5, f32[1,2,8,128,128]{4,3,1,2,0:T(8,128)} %copy-done.3, f32[1,2,8,128,128]{4,3,1,2,0:T(8,128)} %get-tuple-element.21, ...), kind=kLoop, calls=%fused_computation.37 | loop fusion | flops 3145728 | bytes 9437189 | tf_op jit(solution)/shard_map/add | solution.py:44
  64.5 2.3 %collective-permute-start.7 = (f32[1,2,8,128,128]{4,3,1,2,0:T(8,128)}, f32[1,2,8,128,128]{4,3,1,2,0:T(8,128)}, u32[]{:S(2)}, u32[]{:S(2)}) collective-permute-start(f32[1,2,8,128,128]{4,3,1,2,0:T(8,128)} %get-tuple-element.14), channel_id=1, source_target_pairs={{32,48},{96,80},{160,176},{224,208},{33,49},{97,81},{161,177},{225... | collective-permute-start | bytes 3145736 | tf_op jit(solution)/shard_map/ppermute | solution.py:22
  66.8 2.3 %collective-permute-start.8 = (f32[1,2,8,128,128]{4,3,1,2,0:T(8,128)}, f32[1,2,8,128,128]{4,3,1,2,0:T(8,128)}, u32[]{:S(2)}, u32[]{:S(2)}) collective-permute-start(f32[1,2,8,128,128]{4,3,1,2,0:T(8,128)} %get-tuple-element.14), channel_id=1, source_target_pairs={{32,64},{96,112},{160,192},{224,240},{33,65},{97,113},{161,193},{2... | collective-permute-start | bytes 3145736 | tf_op jit(solution)/shard_map/ppermute | solution.py:22
  70.5 1.6 copy.36
  72.1 6.9 %all-to-all-start = ((f32[1,2,8,128,128]{4,2,1,0,3:T(8,128)}), f32[1,2,8,128,128]{4,2,1,0,3:T(8,128)}, u32[]{:S(2)}, u32[]{:S(2)}) async-start(f32[1,2,8,128,128]{4,2,1,0,3:T(8,128)} %copy.36), calls=%async_computation | async-start | bytes 2097152 | tf_op jit(solution)/shard_map/all_to_all | solution.py:95
  79.0 2.4 %add_add_fusion = f32[1,2,8,128,128]{4,3,1,2,0:T(8,128)S(1)} fusion(f32[1,2,8,128,128]{4,3,1,2,0:T(8,128)} %collective-permute-done.8, f32[1,2,8,128,128]{4,3,1,2,0:T(8,128)} %collective-permute-done.7, f32[1,2,8,128,128]{4,3,1,2,0:T(8,128)} %get-tuple-element.14, f32[1,2,8,128,128]{4,3,1,2,0:T(8,128)S(1)} %collective-permute-done.3, ...), kind=kLoop, calls=%fused_computation.35 | loop fusion | flops 1310720 | bytes 6291457 | tf_op jit(solution)/shard_map/add | solution.py:48
  82.8 1.6 copy.50
  84.4 22.8 %all-to-all-done = f32[1,2,8,128,128]{4,2,1,0,3:T(8,128)} async-done(((f32[1,2,8,128,128]{4,2,1,0,3:T(8,128)}), f32[1,2,8,128,128]{4,2,1,0,3:T(8,128)}, u32[]{:S(2)}, u32[]{:S(2)}) %all-to-all-start) | async-done | bytes 1048608 | tf_op jit(solution)/shard_map/all_to_all | solution.py:95
  107.2 4.3 %all-to-all-start.2 = ((f32[1,2,8,128,128]{4,2,1,0,3:T(8,128)}), f32[1,2,8,128,128]{4,2,1,0,3:T(8,128)}, u32[]{:S(2)}, u32[]{:S(2)}) async-start(f32[1,2,8,128,128]{4,2,1,0,3:T(8,128)} %copy.50), calls=%async_computation.2 | async-start | bytes 2097152 | tf_op jit(solution)/shard_map/all_to_all | solution.py:95
  112.3 2.8 %convolution_bitcast_fusion.10 = f32[1,2,128,8,128]{4,2,3,1,0:T(8,128)} fusion(f32[1,2,8,16,8,128]{5,2,1,4,3,0:T(8,128)} %bitcast.23, f32[1,128,2,128]{1,3,0,2:T(8,128)S(1)} %get-tuple-element.28, f32[1,128,2,128]{1,3,0,2:T(8,128)S(1)} %get-tuple-element.31), kind=kOutput, calls=%fused_computation.10 | convolution fusion | flops 402718720 | bytes 2359296 | tf_op jit(solution)/shard_map/prnbc,rntk->ptkbc/dot_general | solution.py:64
  115.1 24.1 %all-to-all-done.2 = f32[1,2,8,128,128]{4,2,1,0,3:T(8,128)} async-done(((f32[1,2,8,128,128]{4,2,1,0,3:T(8,128)}), f32[1,2,8,128,128]{4,2,1,0,3:T(8,128)}, u32[]{:S(2)}, u32[]{:S(2)}) %all-to-all-start.2) | async-done | bytes 1048608 | tf_op jit(solution)/shard_map/all_to_all | solution.py:95
  139.2 2.0 convolution_bitcast_fusion.5
  143.7 4.5 %all-to-all-start.1 = ((f32[1,2,128,8,128]{4,3,1,0,2:T(8,128)}), f32[1,2,128,8,128]{4,3,1,0,2:T(8,128)}, u32[]{:S(2)}, u32[]{:S(2)}) async-start(f32[1,2,128,8,128]{4,3,1,0,2:T(8,128)} %copy.41), calls=%async_computation.1 | async-start | bytes 2097152 | tf_op jit(solution)/shard_map/all_to_all | solution.py:101
  148.9 1.6 copy.54
  150.4 22.1 %all-to-all-done.1 = f32[1,2,128,8,128]{4,3,1,0,2:T(8,128)} async-done(((f32[1,2,128,8,128]{4,3,1,0,2:T(8,128)}), f32[1,2,128,8,128]{4,3,1,0,2:T(8,128)}, u32[]{:S(2)}, u32[]{:S(2)}) %all-to-all-start.1) | async-done | bytes 1048608 | tf_op jit(solution)/shard_map/all_to_all | solution.py:101
  172.5 3.7 %all-to-all-start.3 = ((f32[1,2,128,8,128]{4,3,1,0,2:T(8,128)}), f32[1,2,128,8,128]{4,3,1,0,2:T(8,128)S(1)}, u32[]{:S(2)}, u32[]{:S(2)}) async-start(f32[1,2,128,8,128]{4,3,1,0,2:T(8,128)} %copy.54), calls=%async_computation.3 | async-start | bytes 2097152 | tf_op jit(solution)/shard_map/all_to_all | solution.py:101
  176.2 2.8 %convolution_bitcast_fusion.8 = f32[2,8,128,128,1]{3,2,1,0,4:T(8,128)} fusion(f32[1,2,16,8,8,128]{5,4,1,3,2,0:T(8,128)} %bitcast.39, f32[2,128,2,128,1]{1,3,2,0,4:T(8,128)S(1)} %get-tuple-element.26), kind=kOutput, calls=%fused_computation.8 | convolution fusion | flops 402653184 | bytes 2359296 | tf_op jit(solution)/shard_map/pranc,rntk->ptakc/dot_general | solution.py:64
  179.0 15.1 %all-to-all-done.3 = f32[1,2,128,8,128]{4,3,1,0,2:T(8,128)S(1)} async-done(((f32[1,2,128,8,128]{4,3,1,0,2:T(8,128)}), f32[1,2,128,8,128]{4,3,1,0,2:T(8,128)S(1)}, u32[]{:S(2)}, u32[]{:S(2)}) %all-to-all-start.3) | async-done | bytes 1048608 | tf_op jit(solution)/shard_map/all_to_all | solution.py:101
  (50 shorter events, 18.3 us)
Async XLA Ops:
  2.4 4.4 %collective-permute-start.1 = (f32[1,2,8,128,128]{4,3,1,2,0:T(8,128)}, f32[1,2,8,128,128]{4,3,1,2,0:T(8,128)S(1)}, u32[]{:S(2)}, u32[]{:S(2)}) collective-permute-start(f32[1,2,8,128,128]{4,3,1,2,0:T(8,128)} %get-tuple-element.21), channel_id=1, source_target_pairs={{0,32},{128,160},{1,33},{129,161},{2,34},{130,162},{3,35},{131,163... | collective-permute-start | bytes 3145736 | tf_op jit(solution)/shard_map/ppermute | solution.py:22
  3.2 18.1 %collective-permute-start.2 = (f32[1,2,8,128,128]{4,3,1,2,0:T(8,128)}, f32[1,2,8,128,128]{4,3,1,2,0:T(8,128)S(1)}, u32[]{:S(2)}, u32[]{:S(2)}) collective-permute-start(f32[1,2,8,128,128]{4,3,1,2,0:T(8,128)} %get-tuple-element.21), channel_id=1, source_target_pairs={{0,96},{128,224},{1,97},{129,225},{2,98},{130,226},{3,99},{131,227... | collective-permute-start | bytes 3145736 | tf_op jit(solution)/shard_map/ppermute | solution.py:22
  4.5 16.8 %collective-permute-start.3 = (f32[1,2,8,128,128]{4,3,1,2,0:T(8,128)S(1)}, f32[1,2,8,128,128]{4,3,1,2,0:T(8,128)S(1)}, u32[]{:S(2)}, u32[]{:S(2)}) collective-permute-start(f32[1,2,8,128,128]{4,3,1,2,0:T(8,128)S(1)} %get-tuple-element.22), channel_id=1, source_target_pairs={{0,128},{128,0},{1,129},{129,1},{2,130},{130,2},{3,131},{131,3},{4... | collective-permute-start | bytes 3145736 | tf_op jit(solution)/shard_map/ppermute | solution.py:35
  5.2 23.6 %collective-permute-start = (f32[1,2,8,128,128]{4,3,1,2,0:T(8,128)}, f32[1,2,8,128,128]{4,3,1,2,0:T(8,128)}, u32[]{:S(2)}, u32[]{:S(2)}) collective-permute-start(f32[1,2,8,128,128]{4,3,1,2,0:T(8,128)} %get-tuple-element.21), channel_id=1, source_target_pairs={{0,16},{128,144},{1,17},{129,145},{2,18},{130,146},{3,19},{131,147... | collective-permute-start | bytes 3145736 | tf_op jit(solution)/shard_map/ppermute | solution.py:22
  6.8 15.8 %copy-start.4 = (f32[1,2,8,128,128]{4,3,1,2,0:T(8,128)}, f32[1,2,8,128,128]{4,3,1,2,0:T(8,128)S(1)}, u32[]{:S(2)}) copy-start(f32[1,2,8,128,128]{4,3,1,2,0:T(8,128)S(1)} %collective-permute-done.1) | copy-start | bytes 3145732
  21.3 1.3 copy-start.5
  22.6 6.2 %collective-permute-start.4 = (f32[1,2,8,128,128]{4,3,1,2,0:T(8,128)}, f32[1,2,8,128,128]{4,3,1,2,0:T(8,128)S(1)}, u32[]{:S(2)}, u32[]{:S(2)}) collective-permute-start(f32[1,2,8,128,128]{4,3,1,2,0:T(8,128)} %add_add_fusion.2), channel_id=1, source_target_pairs={{32,48},{96,112},{0,16},{160,176},{224,240},{128,144},{33,49},{97,... | collective-permute-start | bytes 3145736 | tf_op jit(solution)/shard_map/ppermute | solution.py:22
  24.0 4.9 %collective-permute-start.5 = (f32[1,2,8,128,128]{4,3,1,2,0:T(8,128)}, f32[1,2,8,128,128]{4,3,1,2,0:T(8,128)}, u32[]{:S(2)}, u32[]{:S(2)}) collective-permute-start(f32[1,2,8,128,128]{4,3,1,2,0:T(8,128)} %add_add_fusion.2), channel_id=1, source_target_pairs={{32,64},{0,32},{160,192},{128,160},{33,65},{1,33},{161,193},{129,1... | collective-permute-start | bytes 3145736 | tf_op jit(solution)/shard_map/ppermute | solution.py:22
  25.6 34.2 %collective-permute-start.6 = (f32[1,2,8,128,128]{4,3,1,2,0:T(8,128)}, f32[1,2,8,128,128]{4,3,1,2,0:T(8,128)}, u32[]{:S(2)}, u32[]{:S(2)}) collective-permute-start(f32[1,2,8,128,128]{4,3,1,2,0:T(8,128)} %add_add_fusion.2), channel_id=1, source_target_pairs={{96,80},{0,96},{224,208},{128,224},{97,81},{1,97},{225,209},{129,2... | collective-permute-start | bytes 3145736 | tf_op jit(solution)/shard_map/ppermute | solution.py:22
  28.8 1.0 copy-start.3
  64.5 14.5 %collective-permute-start.7 = (f32[1,2,8,128,128]{4,3,1,2,0:T(8,128)}, f32[1,2,8,128,128]{4,3,1,2,0:T(8,128)}, u32[]{:S(2)}, u32[]{:S(2)}) collective-permute-start(f32[1,2,8,128,128]{4,3,1,2,0:T(8,128)} %get-tuple-element.14), channel_id=1, source_target_pairs={{32,48},{96,80},{160,176},{224,208},{33,49},{97,81},{161,177},{225... | collective-permute-start | bytes 3145736 | tf_op jit(solution)/shard_map/ppermute | solution.py:22
  66.8 12.2 %collective-permute-start.8 = (f32[1,2,8,128,128]{4,3,1,2,0:T(8,128)}, f32[1,2,8,128,128]{4,3,1,2,0:T(8,128)}, u32[]{:S(2)}, u32[]{:S(2)}) collective-permute-start(f32[1,2,8,128,128]{4,3,1,2,0:T(8,128)} %get-tuple-element.14), channel_id=1, source_target_pairs={{32,64},{96,112},{160,192},{224,240},{33,65},{97,113},{161,193},{2... | collective-permute-start | bytes 3145736 | tf_op jit(solution)/shard_map/ppermute | solution.py:22
  72.1 35.1 %all-to-all-start = ((f32[1,2,8,128,128]{4,2,1,0,3:T(8,128)}), f32[1,2,8,128,128]{4,2,1,0,3:T(8,128)}, u32[]{:S(2)}, u32[]{:S(2)}) async-start(f32[1,2,8,128,128]{4,2,1,0,3:T(8,128)} %copy.36), calls=%async_computation | async-start | bytes 2097152 | tf_op jit(solution)/shard_map/all_to_all | solution.py:95
  79.0 2.4 %copy-start = (f32[1,2,8,128,128]{4,3,2,1,0:T(8,128)S(1)}, f32[1,2,8,128,128]{4,3,2,1,0:T(8,128)}, u32[]{:S(2)}) copy-start(f32[1,2,8,128,128]{4,3,2,1,0:T(8,128)} %param.2) | copy-start | bytes 3145732
  84.4 27.2 %copy-start.8 = (f32[1,128,2,128]{1,3,2,0:T(8,128)S(1)}, f32[1,128,2,128]{1,3,2,0:T(8,128)}, u32[]{:S(2)}) copy-start(f32[1,128,2,128]{1,3,2,0:T(8,128)} %get-tuple-element.32) | copy-start | bytes 393220
  107.2 32.0 %all-to-all-start.2 = ((f32[1,2,8,128,128]{4,2,1,0,3:T(8,128)}), f32[1,2,8,128,128]{4,2,1,0,3:T(8,128)}, u32[]{:S(2)}, u32[]{:S(2)}) async-start(f32[1,2,8,128,128]{4,2,1,0,3:T(8,128)} %copy.50), calls=%async_computation.2 | async-start | bytes 2097152 | tf_op jit(solution)/shard_map/all_to_all | solution.py:95
  139.2 2.0 copy-start.2
  139.2 2.0 copy-start.7
  143.7 28.8 %all-to-all-start.1 = ((f32[1,2,128,8,128]{4,3,1,0,2:T(8,128)}), f32[1,2,128,8,128]{4,3,1,0,2:T(8,128)}, u32[]{:S(2)}, u32[]{:S(2)}) async-start(f32[1,2,128,8,128]{4,3,1,0,2:T(8,128)} %copy.41), calls=%async_computation.1 | async-start | bytes 2097152 | tf_op jit(solution)/shard_map/all_to_all | solution.py:101
  172.5 21.5 %all-to-all-start.3 = ((f32[1,2,128,8,128]{4,3,1,0,2:T(8,128)}), f32[1,2,128,8,128]{4,3,1,0,2:T(8,128)S(1)}, u32[]{:S(2)}, u32[]{:S(2)}) async-start(f32[1,2,128,8,128]{4,3,1,0,2:T(8,128)} %copy.54), calls=%async_computation.3 | async-start | bytes 2097152 | tf_op jit(solution)/shard_map/all_to_all | solution.py:101
  194.1 1.2 copy-start.1
  194.1 1.3 copy-start.6

commit v3 on v0

--- a/solution.py
+++ b/solution.py
@@ -5,10 +5,10 @@
 from jax import lax
 from jax.sharding import PartitionSpec as P
 
+
 NX = 128
 NY = 128
 NZ = 128
-STEPS = 2
 
 
 fused_forms = {1: "prnbc,rntk->ptkbc", 2: "pranc,rntk->ptakc", 3: "prabn,rntk->ptabk"}
@@ -40,7 +40,9 @@
     head = index % 8 == 0
     own = jnp.where(head, bands, 0).astype(bands.dtype)
     crossed = lax.ppermute(bands, axis, [(0, 8), (8, 0)])
-    return [own + half_tree(own, axis), crossed + half_tree(crossed, axis)]
+    own = own + half_tree(own, axis)
+    crossed = crossed + half_tree(crossed, axis)
+    return [own, crossed]
 
 
 def dft_tables(length):

time: 192 us -> 192 us (level)
  no operation moved by 1% of the time
where the time goes in v3:
time: 192 us; the launch traced here: 190 us
  waiting for transfers between devices  113 us (59%)
  starting transfers between devices  44.8 us (23%)
  matrix products  14.5 us (8%)
  other arithmetic  9.97 us (5%)
  local copies, waits for them, and re-layouts  7.43 us (4%)
    all_to_all x2, waiting for transfers between devices, body(): lax.all_to_all(stacked, 'grid', split_axis=3, concat_axis=2, tiled=True)  45.7 us
    all_to_all x2, waiting for transfers between devices, body(): lax.all_to_all(back, 'grid', split_axis=2, concat_axis=3, tiled=True)  37.6 us
    ppermute x12, waiting for transfers between devices, send(): lax.ppermute(operand, axis, [(band_place(h, *a), band_place(h, *b)) for h...  29.9 us
    all_to_all x2, starting transfers between devices, body(): lax.all_to_all(stacked, 'grid', split_axis=3, concat_axis=2, tiled=True)  18.9 us
    ppermute x12, starting transfers between devices, send(): lax.ppermute(operand, axis, [(band_place(h, *a), band_place(h, *b)) for h...  16 us
    dot_general x12, matrix products, transform(): jnp.einsum(fused_forms[axis_dim], values, table, precision=lax.Precision....  14.5 us
    all_to_all x2, starting transfers between devices, body(): lax.all_to_all(back, 'grid', split_axis=2, concat_axis=3, tiled=True)  8.17 us
    transpose x4, local copies, waits for them, and re-layouts, transform(): jnp.einsum(fused_forms[axis_dim], values, table, precision=lax.Precision....  6.34 us
  transfers between devices with their start and end apart: 17, of which 6 were waited for; matrix products, arithmetic and copies ran while one was open for 11% of the time, Pallas kernels for 0%

profile of v3, /device:TPU:24, one launch (start us, length us, event | category | flops | bytes accessed | tf_op | source)
XLA Modules:
  0.0 190.1 jit_solution(902207428888958431)
XLA Ops:
  1.5 1.6 collective-permute-start.6
  7.9 18.3 %collective-permute-done.2 = f32[1,2,8,128,128]{4,3,1,2,0:T(8,128)S(1)} collective-permute-done((f32[1,2,8,128,128]{4,3,1,2,0:T(8,128)S(1)}, f32[1,2,8,128,128]{4,3,1,2,0:T(8,128)S(1)}, u32[]{:S(2)}, u32[]{:S(2)}) %collective-permute-start.2) | collective-permute-done | bytes 1048608 | tf_op jit(solution)/shard_map/ppermute | solution.py:23
  30.4 11.6 %collective-permute-done.9 = f32[1,2,8,128,128]{4,3,1,2,0:T(8,128)S(1)} collective-permute-done((f32[1,2,8,128,128]{4,3,1,2,0:T(8,128)}, f32[1,2,8,128,128]{4,3,1,2,0:T(8,128)S(1)}, u32[]{:S(2)}, u32[]{:S(2)}) %collective-permute-start.9) | collective-permute-done | bytes 1048608 | tf_op jit(solution)/shard_map/ppermute | solution.py:23
  42.0 1.6 collective-permute-start.7
  44.7 2.3 %collective-permute-start.12 = (f32[1,2,8,128,128]{4,3,1,2,0:T(8,128)}, f32[1,2,8,128,128]{4,3,1,2,0:T(8,128)}, u32[]{:S(2)}, u32[]{:S(2)}) collective-permute-start(f32[1,2,8,128,128]{4,3,1,2,0:T(8,128)} %add.131), channel_id=1, source_target_pairs={{96,80},{224,208},{97,81},{225,209},{98,82},{226,210},{99,83},{227... | collective-permute-start | bytes 3145736 | tf_op jit(solution)/shard_map/ppermute | solution.py:23
  47.0 1.7 collective-permute-start.11
  48.6 2.3 %collective-permute-start.10 = (f32[1,2,8,128,128]{4,3,1,2,0:T(8,128)}, f32[1,2,8,128,128]{4,3,1,2,0:T(8,128)}, u32[]{:S(2)}, u32[]{:S(2)}) collective-permute-start(f32[1,2,8,128,128]{4,3,1,2,0:T(8,128)} %add.131), channel_id=1, source_target_pairs={{32,48},{96,112},{160,176},{224,240},{33,49},{97,113},{161,177},{2... | collective-permute-start | bytes 3145736 | tf_op jit(solution)/shard_map/ppermute | solution.py:23
  52.9 1.6 copy.35
  54.5 14.6 %all-to-all-start = ((f32[1,2,8,128,128]{4,2,1,0,3:T(8,128)}), f32[1,2,8,128,128]{4,2,1,0,3:T(8,128)}, u32[]{:S(2)}, u32[]{:S(2)}) async-start(f32[1,2,8,128,128]{4,2,1,0,3:T(8,128)} %copy.35), calls=%async_computation | async-start | bytes 2097152 | tf_op jit(solution)/shard_map/all_to_all | solution.py:91
  69.2 3.4 %add_add_fusion = f32[1,2,8,128,128]{4,3,1,2,0:T(8,128)S(1)} fusion(f32[1,2,8,128,128]{4,3,1,2,0:T(8,128)} %collective-permute-done.6, f32[1,2,8,128,128]{4,3,1,2,0:T(8,128)} %collective-permute-done.12, f32[1,2,8,128,128]{4,3,1,2,0:T(8,128)} %collective-permute-done.11, f32[1,2,8,128,128]{4,3,1,2,0:T(8,128)} %collective-permute-done.10, ...), kind=kLoop, calls=%fused_computation.35 | loop fusion | flops 1310720 | bytes 7340032 | tf_op jit(solution)/shard_map/add | solution.py:44
  74.0 1.6 copy.50
  75.6 21.8 %all-to-all-done = f32[1,2,8,128,128]{4,2,1,0,3:T(8,128)} async-done(((f32[1,2,8,128,128]{4,2,1,0,3:T(8,128)}), f32[1,2,8,128,128]{4,2,1,0,3:T(8,128)}, u32[]{:S(2)}, u32[]{:S(2)}) %all-to-all-start) | async-done | bytes 1048608 | tf_op jit(solution)/shard_map/all_to_all | solution.py:91
  97.4 4.3 %all-to-all-start.2 = ((f32[1,2,8,128,128]{4,2,1,0,3:T(8,128)}), f32[1,2,8,128,128]{4,2,1,0,3:T(8,128)}, u32[]{:S(2)}, u32[]{:S(2)}) async-start(f32[1,2,8,128,128]{4,2,1,0,3:T(8,128)} %copy.50), calls=%async_computation.2 | async-start | bytes 2097152 | tf_op jit(solution)/shard_map/all_to_all | solution.py:91
  102.4 2.8 %convolution_bitcast_fusion.10 = f32[1,2,128,8,128]{4,2,3,1,0:T(8,128)} fusion(f32[1,2,8,16,8,128]{5,2,1,4,3,0:T(8,128)} %bitcast.23, f32[1,128,2,128]{1,3,0,2:T(8,128)S(1)} %get-tuple-element.26, f32[1,128,2,128]{1,3,0,2:T(8,128)S(1)} %get-tuple-element.29), kind=kOutput, calls=%fused_computation.10 | convolution fusion | flops 402718720 | bytes 2359296 | tf_op jit(solution)/shard_map/prnbc,rntk->ptkbc/dot_general | solution.py:60
  105.2 23.9 %all-to-all-done.2 = f32[1,2,8,128,128]{4,2,1,0,3:T(8,128)} async-done(((f32[1,2,8,128,128]{4,2,1,0,3:T(8,128)}), f32[1,2,8,128,128]{4,2,1,0,3:T(8,128)}, u32[]{:S(2)}, u32[]{:S(2)}) %all-to-all-start.2) | async-done | bytes 1048608 | tf_op jit(solution)/shard_map/all_to_all | solution.py:91
  129.1 2.0 %convolution_bitcast_fusion.5 = f32[1,2,128,8,128]{4,2,3,1,0:T(8,128)S(1)} fusion(f32[1,2,8,16,8,128]{5,2,1,4,3,0:T(8,128)} %bitcast.68, f32[1,128,2,128]{1,3,0,2:T(8,128)S(1)} %get-tuple-element.26, f32[1,128,2,128]{1,3,0,2:T(8,128)S(1)} %get-tuple-element.29), kind=kOutput, calls=%fused_computation.5 | convolution fusion | flops 402718720 | bytes 2359296 | tf_op jit(solution)/shard_map/prnbc,rntk->ptkbc/dot_general | solution.py:60
  134.6 3.8 %all-to-all-start.3 = ((f32[1,2,128,8,128]{4,3,1,0,2:T(8,128)}), f32[1,2,128,8,128]{4,3,1,0,2:T(8,128)S(1)}, u32[]{:S(2)}, u32[]{:S(2)}) async-start(f32[1,2,128,8,128]{4,3,1,0,2:T(8,128)} %copy.54), calls=%async_computation.3 | async-start | bytes 2097152 | tf_op jit(solution)/shard_map/all_to_all | solution.py:97
  138.5 1.8 convolution_bitcast_fusion.9
  140.3 1.6 copy.40
  141.9 21.2 %all-to-all-done.3 = f32[1,2,128,8,128]{4,3,1,0,2:T(8,128)S(1)} async-done(((f32[1,2,128,8,128]{4,3,1,0,2:T(8,128)}), f32[1,2,128,8,128]{4,3,1,0,2:T(8,128)S(1)}, u32[]{:S(2)}, u32[]{:S(2)}) %all-to-all-start.3) | async-done | bytes 1048608 | tf_op jit(solution)/shard_map/all_to_all | solution.py:97
  163.1 4.3 %all-to-all-start.1 = ((f32[1,2,128,8,128]{4,3,1,0,2:T(8,128)}), f32[1,2,128,8,128]{4,3,1,0,2:T(8,128)}, u32[]{:S(2)}, u32[]{:S(2)}) async-start(f32[1,2,128,8,128]{4,3,1,0,2:T(8,128)} %copy.40), calls=%async_computation.1 | async-start | bytes 2097152 | tf_op jit(solution)/shard_map/all_to_all | solution.py:97
  167.4 1.6 convolution_bitcast_fusion.3
  169.0 16.3 %all-to-all-done.1 = f32[1,2,128,8,128]{4,3,1,0,2:T(8,128)} async-done(((f32[1,2,128,8,128]{4,3,1,0,2:T(8,128)}), f32[1,2,128,8,128]{4,3,1,0,2:T(8,128)}, u32[]{:S(2)}, u32[]{:S(2)}) %all-to-all-start.1) | async-done | bytes 1048608 | tf_op jit(solution)/shard_map/all_to_all | solution.py:97
  185.4 1.9 %convolution_bitcast_fusion.8 = f32[2,8,128,128,1]{3,2,1,0,4:T(8,128)S(1)} fusion(f32[1,2,16,8,8,128]{5,4,1,3,2,0:T(8,128)} %bitcast.39, f32[2,128,2,128,1]{1,3,2,0,4:T(8,128)S(1)} %get-tuple-element.24), kind=kOutput, calls=%fused_computation.8 | convolution fusion | flops 402653184 | bytes 2359296 | tf_op jit(solution)/shard_map/pranc,rntk->ptakc/dot_general | solution.py:60
  (51 shorter events, 21.9 us)
Async XLA Ops:
  1.5 3.7 %collective-permute-start.6 = (f32[1,2,8,128,128]{4,3,1,2,0:T(8,128)S(1)}, f32[1,2,8,128,128]{4,3,1,2,0:T(8,128)}, u32[]{:S(2)}, u32[]{:S(2)}) collective-permute-start(f32[1,2,8,128,128]{4,3,1,2,0:T(8,128)S(1)} %get-tuple-element.20), channel_id=1, source_target_pairs={{0,128},{128,0},{1,129},{129,1},{2,130},{130,2},{3,131},{131,3},{4... | collective-permute-start | bytes 3145736 | tf_op jit(solution)/shard_map/ppermute | solution.py:42
  3.1 4.8 %collective-permute-start.1 = (f32[1,2,8,128,128]{4,3,1,2,0:T(8,128)S(1)}, f32[1,2,8,128,128]{4,3,1,2,0:T(8,128)S(1)}, u32[]{:S(2)}, u32[]{:S(2)}) collective-permute-start(f32[1,2,8,128,128]{4,3,1,2,0:T(8,128)S(1)} %get-tuple-element.19), channel_id=1, source_target_pairs={{0,32},{128,160},{1,33},{129,161},{2,34},{130,162},{3,35},{131,163... | collective-permute-start | bytes 3145736 | tf_op jit(solution)/shard_map/ppermute | solution.py:23
  3.8 22.4 %collective-permute-start.2 = (f32[1,2,8,128,128]{4,3,1,2,0:T(8,128)S(1)}, f32[1,2,8,128,128]{4,3,1,2,0:T(8,128)S(1)}, u32[]{:S(2)}, u32[]{:S(2)}) collective-permute-start(f32[1,2,8,128,128]{4,3,1,2,0:T(8,128)S(1)} %get-tuple-element.19), channel_id=1, source_target_pairs={{0,96},{128,224},{1,97},{129,225},{2,98},{130,226},{3,99},{131,227... | collective-permute-start | bytes 3145736 | tf_op jit(solution)/shard_map/ppermute | solution.py:23
  5.1 23.3 %collective-permute-start.8 = (f32[1,2,8,128,128]{4,3,1,2,0:T(8,128)}, f32[1,2,8,128,128]{4,3,1,2,0:T(8,128)S(1)}, u32[]{:S(2)}, u32[]{:S(2)}) collective-permute-start(f32[1,2,8,128,128]{4,3,1,2,0:T(8,128)} %collective-permute-done.6), channel_id=1, source_target_pairs={{0,32},{128,160},{1,33},{129,161},{2,34},{130,162},{3,35},{131,163... | collective-permute-start | bytes 3145736 | tf_op jit(solution)/shard_map/ppermute | solution.py:23
  5.9 36.1 %collective-permute-start.9 = (f32[1,2,8,128,128]{4,3,1,2,0:T(8,128)}, f32[1,2,8,128,128]{4,3,1,2,0:T(8,128)S(1)}, u32[]{:S(2)}, u32[]{:S(2)}) collective-permute-start(f32[1,2,8,128,128]{4,3,1,2,0:T(8,128)} %collective-permute-done.6), channel_id=1, source_target_pairs={{0,96},{128,224},{1,97},{129,225},{2,98},{130,226},{3,99},{131,227... | collective-permute-start | bytes 3145736 | tf_op jit(solution)/shard_map/ppermute | solution.py:23
  7.2 37.5 %collective-permute-start = (f32[1,2,8,128,128]{4,3,1,2,0:T(8,128)S(1)}, f32[1,2,8,128,128]{4,3,1,2,0:T(8,128)S(1)}, u32[]{:S(2)}, u32[]{:S(2)}) collective-permute-start(f32[1,2,8,128,128]{4,3,1,2,0:T(8,128)S(1)} %get-tuple-element.19), channel_id=1, source_target_pairs={{0,16},{128,144},{1,17},{129,145},{2,18},{130,146},{3,19},{131,147... | collective-permute-start | bytes 3145736 | tf_op jit(solution)/shard_map/ppermute | solution.py:23
  26.3 20.6 %collective-permute-start.5 = (f32[1,2,8,128,128]{4,3,1,2,0:T(8,128)S(1)}, f32[1,2,8,128,128]{4,3,1,2,0:T(8,128)S(1)}, u32[]{:S(2)}, u32[]{:S(2)}) collective-permute-start(f32[1,2,8,128,128]{4,3,1,2,0:T(8,128)S(1)} %add.124), channel_id=1, source_target_pairs={{96,80},{224,208},{97,81},{225,209},{98,82},{226,210},{99,83},{227... | collective-permute-start | bytes 3145736 | tf_op jit(solution)/shard_map/ppermute | solution.py:23
  27.7 20.9 %collective-permute-start.4 = (f32[1,2,8,128,128]{4,3,1,2,0:T(8,128)S(1)}, f32[1,2,8,128,128]{4,3,1,2,0:T(8,128)S(1)}, u32[]{:S(2)}, u32[]{:S(2)}) collective-permute-start(f32[1,2,8,128,128]{4,3,1,2,0:T(8,128)S(1)} %add.124), channel_id=1, source_target_pairs={{32,64},{160,192},{33,65},{161,193},{34,66},{162,194},{35,67},{163... | collective-permute-start | bytes 3145736 | tf_op jit(solution)/shard_map/ppermute | solution.py:23
  28.5 22.5 %collective-permute-start.3 = (f32[1,2,8,128,128]{4,3,1,2,0:T(8,128)S(1)}, f32[1,2,8,128,128]{4,3,1,2,0:T(8,128)S(1)}, u32[]{:S(2)}, u32[]{:S(2)}) collective-permute-start(f32[1,2,8,128,128]{4,3,1,2,0:T(8,128)S(1)} %add.124), channel_id=1, source_target_pairs={{32,48},{96,112},{160,176},{224,240},{33,49},{97,113},{161,177},{2... | collective-permute-start | bytes 3145736 | tf_op jit(solution)/shard_map/ppermute | solution.py:23
  42.0 27.1 %collective-permute-start.7 = (f32[1,2,8,128,128]{4,3,1,2,0:T(8,128)}, f32[1,2,8,128,128]{4,3,1,2,0:T(8,128)}, u32[]{:S(2)}, u32[]{:S(2)}) collective-permute-start(f32[1,2,8,128,128]{4,3,1,2,0:T(8,128)} %collective-permute-done.6), channel_id=1, source_target_pairs={{0,16},{128,144},{1,17},{129,145},{2,18},{130,146},{3,19},{131,147... | collective-permute-start | bytes 3145736 | tf_op jit(solution)/shard_map/ppermute | solution.py:23
  44.7 24.4 %collective-permute-start.12 = (f32[1,2,8,128,128]{4,3,1,2,0:T(8,128)}, f32[1,2,8,128,128]{4,3,1,2,0:T(8,128)}, u32[]{:S(2)}, u32[]{:S(2)}) collective-permute-start(f32[1,2,8,128,128]{4,3,1,2,0:T(8,128)} %add.131), channel_id=1, source_target_pairs={{96,80},{224,208},{97,81},{225,209},{98,82},{226,210},{99,83},{227... | collective-permute-start | bytes 3145736 | tf_op jit(solution)/shard_map/ppermute | solution.py:23
  47.0 22.2 %collective-permute-start.11 = (f32[1,2,8,128,128]{4,3,1,2,0:T(8,128)}, f32[1,2,8,128,128]{4,3,1,2,0:T(8,128)}, u32[]{:S(2)}, u32[]{:S(2)}) collective-permute-start(f32[1,2,8,128,128]{4,3,1,2,0:T(8,128)} %add.131), channel_id=1, source_target_pairs={{32,64},{160,192},{33,65},{161,193},{34,66},{162,194},{35,67},{163... | collective-permute-start | bytes 3145736 | tf_op jit(solution)/shard_map/ppermute | solution.py:23
  48.6 20.5 %collective-permute-start.10 = (f32[1,2,8,128,128]{4,3,1,2,0:T(8,128)}, f32[1,2,8,128,128]{4,3,1,2,0:T(8,128)}, u32[]{:S(2)}, u32[]{:S(2)}) collective-permute-start(f32[1,2,8,128,128]{4,3,1,2,0:T(8,128)} %add.131), channel_id=1, source_target_pairs={{32,48},{96,112},{160,176},{224,240},{33,49},{97,113},{161,177},{2... | collective-permute-start | bytes 3145736 | tf_op jit(solution)/shard_map/ppermute | solution.py:23
  54.5 42.9 %all-to-all-start = ((f32[1,2,8,128,128]{4,2,1,0,3:T(8,128)}), f32[1,2,8,128,128]{4,2,1,0,3:T(8,128)}, u32[]{:S(2)}, u32[]{:S(2)}) async-start(f32[1,2,8,128,128]{4,2,1,0,3:T(8,128)} %copy.35), calls=%async_computation | async-start | bytes 2097152 | tf_op jit(solution)/shard_map/all_to_all | solution.py:91
  69.1 3.5 %copy-start = (f32[1,2,8,128,128]{4,3,2,1,0:T(8,128)S(1)}, f32[1,2,8,128,128]{4,3,2,1,0:T(8,128)}, u32[]{:S(2)}) copy-start(f32[1,2,8,128,128]{4,3,2,1,0:T(8,128)} %param.2) | copy-start | bytes 3145732
  97.4 31.8 %all-to-all-start.2 = ((f32[1,2,8,128,128]{4,2,1,0,3:T(8,128)}), f32[1,2,8,128,128]{4,2,1,0,3:T(8,128)}, u32[]{:S(2)}, u32[]{:S(2)}) async-start(f32[1,2,8,128,128]{4,2,1,0,3:T(8,128)} %copy.50), calls=%async_computation.2 | async-start | bytes 2097152 | tf_op jit(solution)/shard_map/all_to_all | solution.py:91
  129.1 2.0 %copy-start.2 = (f32[1,2,128,8,128]{4,2,3,1,0:T(8,128)S(1)}, f32[1,2,128,8,128]{4,2,3,1,0:T(8,128)}, u32[]{:S(2)}) copy-start(f32[1,2,128,8,128]{4,2,3,1,0:T(8,128)} %convolution_bitcast_fusion.10) | copy-start | bytes 3145732
  129.1 2.0 %copy-start.4 = (f32[128,8,128]{2,1,0:T(8,128)S(1)}, f32[128,8,128]{2,1,0:T(8,128)}, u32[]{:S(2)}) copy-start(f32[128,8,128]{2,1,0:T(8,128)} %param.3) | copy-start | bytes 1572868
  134.6 28.5 %all-to-all-start.3 = ((f32[1,2,128,8,128]{4,3,1,0,2:T(8,128)}), f32[1,2,128,8,128]{4,3,1,0,2:T(8,128)S(1)}, u32[]{:S(2)}, u32[]{:S(2)}) async-start(f32[1,2,128,8,128]{4,3,1,0,2:T(8,128)} %copy.54), calls=%async_computation.3 | async-start | bytes 2097152 | tf_op jit(solution)/shard_map/all_to_all | solution.py:97
  163.1 22.3 %all-to-all-start.1 = ((f32[1,2,128,8,128]{4,3,1,0,2:T(8,128)}), f32[1,2,128,8,128]{4,3,1,0,2:T(8,128)}, u32[]{:S(2)}, u32[]{:S(2)}) async-start(f32[1,2,128,8,128]{4,3,1,0,2:T(8,128)} %copy.40), calls=%async_computation.1 | async-start | bytes 2097152 | tf_op jit(solution)/shard_map/all_to_all | solution.py:97
  185.4 2.0 %copy-start.1 = (f32[2,8,128,128,1]{3,2,1,0,4:T(8,128)S(1)}, f32[2,8,128,128,1]{3,2,1,0,4:T(8,128)}, u32[]{:S(2)}) copy-start(f32[2,8,128,128,1]{3,2,1,0,4:T(8,128)} %convolution_bitcast_fusion.3) | copy-start | bytes 3145732
  185.4 2.0 %copy-start.3 = (f32[2,128,2,128]{1,3,2,0:T(8,128)S(1)}, f32[2,128,2,128]{1,3,2,0:T(8,128)}, u32[]{:S(2)}) copy-start(f32[2,128,2,128]{1,3,2,0:T(8,128)} %get-tuple-element.23) | copy-start | bytes 786436

commit v4 on v0

--- a/solution.py
+++ b/solution.py
@@ -18,9 +18,17 @@
     return half * 8 + row * 2 + core
 
 
-def half_tree(value, axis):
+def half_tree(value, axis, roots=(0, 0)):
     def send(operand, pairs):
-        return lax.ppermute(operand, axis, [(band_place(h, *a), band_place(h, *b)) for h in (0, 1) for a, b in pairs])
+        return lax.ppermute(
+            operand,
+            axis,
+            [
+                (band_place(h, (a[0] + roots[h]) % 4, a[1]), band_place(h, (b[0] + roots[h]) % 4, b[1]))
+                for h in (0, 1)
+                for a, b in pairs
+            ],
+        )
 
     first = [send(value, [((0, 0), (0, 1))]), send(value, [((0, 0), (1, 0))]), send(value, [((0, 0), (3, 0))])]
     relay = first[1] + first[2]
@@ -39,8 +47,8 @@
     index = lax.axis_index(axis)
     head = index % 8 == 0
     own = jnp.where(head, bands, 0).astype(bands.dtype)
-    crossed = lax.ppermute(bands, axis, [(0, 8), (8, 0)])
-    return [own + half_tree(own, axis), crossed + half_tree(crossed, axis)]
+    crossed = lax.ppermute(bands, axis, [(band_place(0, 0, 0), band_place(1, 1, 0)), (band_place(1, 0, 0), band_place(0, 3, 0))])
+    return [own + half_tree(own, axis), crossed + half_tree(crossed, axis, roots=(3, 1))]
 
 
 def dft_tables(length):

time: 192 us -> 212 us (1.10)
  the two profiles are of different devices: /device:TPU:24 before, /device:TPU:16 now
where the time goes in v4:
time: 212 us; the launch traced here: 211 us
  waiting for transfers between devices  135 us (64%)
  starting transfers between devices  43.7 us (21%)
  matrix products  14.5 us (7%)
  other arithmetic  9.97 us (5%)
  local copies, waits for them, and re-layouts  7.43 us (4%)
    all_to_all x2, waiting for transfers between devices, body(): lax.all_to_all(back, 'grid', split_axis=2, concat_axis=3, tiled=True)  49.7 us
    all_to_all x2, waiting for transfers between devices, body(): lax.all_to_all(stacked, 'grid', split_axis=3, concat_axis=2, tiled=True)  43.4 us
    ppermute x12, waiting for transfers between devices, send(): lax.ppermute(operand, axis, [(band_place(h, (a[0] + roots[h]) % 4, a[1]),...  42.1 us
    ppermute x12, starting transfers between devices, send(): lax.ppermute(operand, axis, [(band_place(h, (a[0] + roots[h]) % 4, a[1]),...  21.5 us
    dot_general x12, matrix products, transform(): jnp.einsum(fused_forms[axis_dim], values, table, precision=lax.Precision....  14.5 us
    all_to_all x2, starting transfers between devices, body(): lax.all_to_all(stacked, 'grid', split_axis=3, concat_axis=2, tiled=True)  12.4 us
    all_to_all x2, starting transfers between devices, body(): lax.all_to_all(back, 'grid', split_axis=2, concat_axis=3, tiled=True)  8.17 us
    transpose x4, local copies, waits for them, and re-layouts, transform(): jnp.einsum(fused_forms[axis_dim], values, table, precision=lax.Precision....  6.34 us
  transfers between devices with their start and end apart: 17, of which 5 were waited for; matrix products, arithmetic and copies ran while one was open for 10% of the time, Pallas kernels for 0%

profile of v4, /device:TPU:16, one launch (start us, length us, event | category | flops | bytes accessed | tf_op | source)
XLA Modules:
  0.0 211.2 jit_solution(3956792550343813837)
XLA Ops:
  1.5 1.6 collective-permute-start.6
  10.9 42.0 %collective-permute-done.9 = f32[1,2,8,128,128]{4,3,1,2,0:T(8,128)S(1)} collective-permute-done((f32[1,2,8,128,128]{4,3,1,2,0:T(8,128)}, f32[1,2,8,128,128]{4,3,1,2,0:T(8,128)S(1)}, u32[]{:S(2)}, u32[]{:S(2)}) %collective-permute-start.9) | collective-permute-done | bytes 1048608 | tf_op jit(solution)/shard_map/ppermute | solution.py:23
  52.9 1.6 collective-permute-start.7
  55.6 2.3 %collective-permute-start.12 = (f32[1,2,8,128,128]{4,3,1,2,0:T(8,128)}, f32[1,2,8,128,128]{4,3,1,2,0:T(8,128)}, u32[]{:S(2)}, u32[]{:S(2)}) collective-permute-start(f32[1,2,8,128,128]{4,3,1,2,0:T(8,128)} %add.131), channel_id=1, source_target_pairs={{64,48},{128,240},{65,49},{129,241},{66,50},{130,242},{67,51},{131... | collective-permute-start | bytes 3145736 | tf_op jit(solution)/shard_map/ppermute | solution.py:23
  57.9 1.7 collective-permute-start.11
  59.6 9.0 %collective-permute-start.10 = (f32[1,2,8,128,128]{4,3,1,2,0:T(8,128)}, f32[1,2,8,128,128]{4,3,1,2,0:T(8,128)}, u32[]{:S(2)}, u32[]{:S(2)}) collective-permute-start(f32[1,2,8,128,128]{4,3,1,2,0:T(8,128)} %add.131), channel_id=1, source_target_pairs={{0,16},{64,80},{192,208},{128,144},{1,17},{65,81},{193,209},{129,1... | collective-permute-start | bytes 3145736 | tf_op jit(solution)/shard_map/ppermute | solution.py:23
  70.6 1.6 copy.35
  72.2 8.1 %all-to-all-start = ((f32[1,2,8,128,128]{4,2,1,0,3:T(8,128)}), f32[1,2,8,128,128]{4,2,1,0,3:T(8,128)}, u32[]{:S(2)}, u32[]{:S(2)}) async-start(f32[1,2,8,128,128]{4,2,1,0,3:T(8,128)} %copy.35), calls=%async_computation | async-start | bytes 2097152 | tf_op jit(solution)/shard_map/all_to_all | solution.py:97
  80.3 3.4 %add_add_fusion = f32[1,2,8,128,128]{4,3,1,2,0:T(8,128)S(1)} fusion(f32[1,2,8,128,128]{4,3,1,2,0:T(8,128)} %collective-permute-done.6, f32[1,2,8,128,128]{4,3,1,2,0:T(8,128)} %collective-permute-done.12, f32[1,2,8,128,128]{4,3,1,2,0:T(8,128)} %collective-permute-done.11, f32[1,2,8,128,128]{4,3,1,2,0:T(8,128)} %collective-permute-done.10, ...), kind=kLoop, calls=%fused_computation.35 | loop fusion | flops 1310720 | bytes 7340032 | tf_op jit(solution)/shard_map/add | solution.py:51
  85.2 1.6 copy.50
  86.8 19.9 %all-to-all-done = f32[1,2,8,128,128]{4,2,1,0,3:T(8,128)} async-done(((f32[1,2,8,128,128]{4,2,1,0,3:T(8,128)}), f32[1,2,8,128,128]{4,2,1,0,3:T(8,128)}, u32[]{:S(2)}, u32[]{:S(2)}) %all-to-all-start) | async-done | bytes 1048608 | tf_op jit(solution)/shard_map/all_to_all | solution.py:97
  106.6 4.3 %all-to-all-start.2 = ((f32[1,2,8,128,128]{4,2,1,0,3:T(8,128)}), f32[1,2,8,128,128]{4,2,1,0,3:T(8,128)}, u32[]{:S(2)}, u32[]{:S(2)}) async-start(f32[1,2,8,128,128]{4,2,1,0,3:T(8,128)} %copy.50), calls=%async_computation.2 | async-start | bytes 2097152 | tf_op jit(solution)/shard_map/all_to_all | solution.py:97
  111.7 2.8 %convolution_bitcast_fusion.10 = f32[1,2,128,8,128]{4,2,3,1,0:T(8,128)} fusion(f32[1,2,8,16,8,128]{5,2,1,4,3,0:T(8,128)} %bitcast.23, f32[1,128,2,128]{1,3,0,2:T(8,128)S(1)} %get-tuple-element.26, f32[1,128,2,128]{1,3,0,2:T(8,128)S(1)} %get-tuple-element.29), kind=kOutput, calls=%fused_computation.10 | convolution fusion | flops 402718720 | bytes 2359296 | tf_op jit(solution)/shard_map/prnbc,rntk->ptkbc/dot_general | solution.py:66
  114.5 23.5 %all-to-all-done.2 = f32[1,2,8,128,128]{4,2,1,0,3:T(8,128)} async-done(((f32[1,2,8,128,128]{4,2,1,0,3:T(8,128)}), f32[1,2,8,128,128]{4,2,1,0,3:T(8,128)}, u32[]{:S(2)}, u32[]{:S(2)}) %all-to-all-start.2) | async-done | bytes 1048608 | tf_op jit(solution)/shard_map/all_to_all | solution.py:97
  138.0 2.0 convolution_bitcast_fusion.5
  141.9 1.6 copy.54
  143.5 3.8 %all-to-all-start.3 = ((f32[1,2,128,8,128]{4,3,1,0,2:T(8,128)}), f32[1,2,128,8,128]{4,3,1,0,2:T(8,128)S(1)}, u32[]{:S(2)}, u32[]{:S(2)}) async-start(f32[1,2,128,8,128]{4,3,1,0,2:T(8,128)} %copy.54), calls=%async_computation.3 | async-start | bytes 2097152 | tf_op jit(solution)/shard_map/all_to_all | solution.py:103
  147.3 1.8 convolution_bitcast_fusion.9
  149.1 1.6 copy.40
  150.7 24.1 %all-to-all-done.3 = f32[1,2,128,8,128]{4,3,1,0,2:T(8,128)S(1)} async-done(((f32[1,2,128,8,128]{4,3,1,0,2:T(8,128)}), f32[1,2,128,8,128]{4,3,1,0,2:T(8,128)S(1)}, u32[]{:S(2)}, u32[]{:S(2)}) %all-to-all-start.3) | async-done | bytes 1048608 | tf_op jit(solution)/shard_map/all_to_all | solution.py:103
  174.9 4.3 %all-to-all-start.1 = ((f32[1,2,128,8,128]{4,3,1,0,2:T(8,128)}), f32[1,2,128,8,128]{4,3,1,0,2:T(8,128)}, u32[]{:S(2)}, u32[]{:S(2)}) async-start(f32[1,2,128,8,128]{4,3,1,0,2:T(8,128)} %copy.40), calls=%async_computation.1 | async-start | bytes 2097152 | tf_op jit(solution)/shard_map/all_to_all | solution.py:103
  179.2 1.6 convolution_bitcast_fusion.3
  180.8 25.6 %all-to-all-done.1 = f32[1,2,128,8,128]{4,3,1,0,2:T(8,128)} async-done(((f32[1,2,128,8,128]{4,3,1,0,2:T(8,128)}), f32[1,2,128,8,128]{4,3,1,0,2:T(8,128)}, u32[]{:S(2)}, u32[]{:S(2)}) %all-to-all-start.1) | async-done | bytes 1048608 | tf_op jit(solution)/shard_map/all_to_all | solution.py:103
  206.4 1.9 convolution_bitcast_fusion.8
  (51 shorter events, 19.0 us)
Async XLA Ops:
  1.5 3.1 %collective-permute-start.6 = (f32[1,2,8,128,128]{4,3,1,2,0:T(8,128)S(1)}, f32[1,2,8,128,128]{4,3,1,2,0:T(8,128)}, u32[]{:S(2)}, u32[]{:S(2)}) collective-permute-start(f32[1,2,8,128,128]{4,3,1,2,0:T(8,128)S(1)} %get-tuple-element.20), channel_id=1, source_target_pairs={{0,160},{128,96},{1,161},{129,97},{2,162},{130,98},{3,163},{131,99... | collective-permute-start | bytes 3145736 | tf_op jit(solution)/shard_map/ppermute | solution.py:50
  3.1 4.2 %collective-permute-start.1 = (f32[1,2,8,128,128]{4,3,1,2,0:T(8,128)S(1)}, f32[1,2,8,128,128]{4,3,1,2,0:T(8,128)S(1)}, u32[]{:S(2)}, u32[]{:S(2)}) collective-permute-start(f32[1,2,8,128,128]{4,3,1,2,0:T(8,128)S(1)} %get-tuple-element.19), channel_id=1, source_target_pairs={{0,32},{128,160},{1,33},{129,161},{2,34},{130,162},{3,35},{131,163... | collective-permute-start | bytes 3145736 | tf_op jit(solution)/shard_map/ppermute | solution.py:23
  3.8 3.5 %collective-permute-start.2 = (f32[1,2,8,128,128]{4,3,1,2,0:T(8,128)S(1)}, f32[1,2,8,128,128]{4,3,1,2,0:T(8,128)S(1)}, u32[]{:S(2)}, u32[]{:S(2)}) collective-permute-start(f32[1,2,8,128,128]{4,3,1,2,0:T(8,128)S(1)} %get-tuple-element.19), channel_id=1, source_target_pairs={{0,96},{128,224},{1,97},{129,225},{2,98},{130,226},{3,99},{131,227... | collective-permute-start | bytes 3145736 | tf_op jit(solution)/shard_map/ppermute | solution.py:23
  4.6 5.0 %collective-permute-start.8 = (f32[1,2,8,128,128]{4,3,1,2,0:T(8,128)}, f32[1,2,8,128,128]{4,3,1,2,0:T(8,128)S(1)}, u32[]{:S(2)}, u32[]{:S(2)}) collective-permute-start(f32[1,2,8,128,128]{4,3,1,2,0:T(8,128)} %collective-permute-done.6), channel_id=1, source_target_pairs={{96,0},{160,192},{97,1},{161,193},{98,2},{162,194},{99,3},{163,195... | collective-permute-start | bytes 3145736 | tf_op jit(solution)/shard_map/ppermute | solution.py:23
  5.3 47.6 %collective-permute-start.9 = (f32[1,2,8,128,128]{4,3,1,2,0:T(8,128)}, f32[1,2,8,128,128]{4,3,1,2,0:T(8,128)S(1)}, u32[]{:S(2)}, u32[]{:S(2)}) collective-permute-start(f32[1,2,8,128,128]{4,3,1,2,0:T(8,128)} %collective-permute-done.6), channel_id=1, source_target_pairs={{96,64},{160,128},{97,65},{161,129},{98,66},{162,130},{99,67},{163... | collective-permute-start | bytes 3145736 | tf_op jit(solution)/shard_map/ppermute | solution.py:23
  6.6 49.0 %collective-permute-start = (f32[1,2,8,128,128]{4,3,1,2,0:T(8,128)S(1)}, f32[1,2,8,128,128]{4,3,1,2,0:T(8,128)S(1)}, u32[]{:S(2)}, u32[]{:S(2)}) collective-permute-start(f32[1,2,8,128,128]{4,3,1,2,0:T(8,128)S(1)} %get-tuple-element.19), channel_id=1, source_target_pairs={{0,16},{128,144},{1,17},{129,145},{2,18},{130,146},{3,19},{131,147... | collective-permute-start | bytes 3145736 | tf_op jit(solution)/shard_map/ppermute | solution.py:23
  7.5 50.4 %collective-permute-start.5 = (f32[1,2,8,128,128]{4,3,1,2,0:T(8,128)S(1)}, f32[1,2,8,128,128]{4,3,1,2,0:T(8,128)S(1)}, u32[]{:S(2)}, u32[]{:S(2)}) collective-permute-start(f32[1,2,8,128,128]{4,3,1,2,0:T(8,128)S(1)} %add.124), channel_id=1, source_target_pairs={{96,80},{224,208},{97,81},{225,209},{98,82},{226,210},{99,83},{227... | collective-permute-start | bytes 3145736 | tf_op jit(solution)/shard_map/ppermute | solution.py:23
  8.2 51.3 %collective-permute-start.4 = (f32[1,2,8,128,128]{4,3,1,2,0:T(8,128)S(1)}, f32[1,2,8,128,128]{4,3,1,2,0:T(8,128)S(1)}, u32[]{:S(2)}, u32[]{:S(2)}) collective-permute-start(f32[1,2,8,128,128]{4,3,1,2,0:T(8,128)S(1)} %add.124), channel_id=1, source_target_pairs={{32,64},{160,192},{33,65},{161,193},{34,66},{162,194},{35,67},{163... | collective-permute-start | bytes 3145736 | tf_op jit(solution)/shard_map/ppermute | solution.py:23
  9.6 59.0 %collective-permute-start.3 = (f32[1,2,8,128,128]{4,3,1,2,0:T(8,128)S(1)}, f32[1,2,8,128,128]{4,3,1,2,0:T(8,128)S(1)}, u32[]{:S(2)}, u32[]{:S(2)}) collective-permute-start(f32[1,2,8,128,128]{4,3,1,2,0:T(8,128)S(1)} %add.124), channel_id=1, source_target_pairs={{32,48},{96,112},{160,176},{224,240},{33,49},{97,113},{161,177},{2... | collective-permute-start | bytes 3145736 | tf_op jit(solution)/shard_map/ppermute | solution.py:23
  52.9 27.4 %collective-permute-start.7 = (f32[1,2,8,128,128]{4,3,1,2,0:T(8,128)}, f32[1,2,8,128,128]{4,3,1,2,0:T(8,128)}, u32[]{:S(2)}, u32[]{:S(2)}) collective-permute-start(f32[1,2,8,128,128]{4,3,1,2,0:T(8,128)} %collective-permute-done.6), channel_id=1, source_target_pairs={{96,112},{160,176},{97,113},{161,177},{98,114},{162,178},{99,115},... | collective-permute-start | bytes 3145736 | tf_op jit(solution)/shard_map/ppermute | solution.py:23
  55.6 24.7 %collective-permute-start.12 = (f32[1,2,8,128,128]{4,3,1,2,0:T(8,128)}, f32[1,2,8,128,128]{4,3,1,2,0:T(8,128)}, u32[]{:S(2)}, u32[]{:S(2)}) collective-permute-start(f32[1,2,8,128,128]{4,3,1,2,0:T(8,128)} %add.131), channel_id=1, source_target_pairs={{64,48},{128,240},{65,49},{129,241},{66,50},{130,242},{67,51},{131... | collective-permute-start | bytes 3145736 | tf_op jit(solution)/shard_map/ppermute | solution.py:23
  57.9 22.4 %collective-permute-start.11 = (f32[1,2,8,128,128]{4,3,1,2,0:T(8,128)}, f32[1,2,8,128,128]{4,3,1,2,0:T(8,128)}, u32[]{:S(2)}, u32[]{:S(2)}) collective-permute-start(f32[1,2,8,128,128]{4,3,1,2,0:T(8,128)} %add.131), channel_id=1, source_target_pairs={{0,32},{192,224},{1,33},{193,225},{2,34},{194,226},{3,35},{195,227... | collective-permute-start | bytes 3145736 | tf_op jit(solution)/shard_map/ppermute | solution.py:23
  59.6 20.7 %collective-permute-start.10 = (f32[1,2,8,128,128]{4,3,1,2,0:T(8,128)}, f32[1,2,8,128,128]{4,3,1,2,0:T(8,128)}, u32[]{:S(2)}, u32[]{:S(2)}) collective-permute-start(f32[1,2,8,128,128]{4,3,1,2,0:T(8,128)} %add.131), channel_id=1, source_target_pairs={{0,16},{64,80},{192,208},{128,144},{1,17},{65,81},{193,209},{129,1... | collective-permute-start | bytes 3145736 | tf_op jit(solution)/shard_map/ppermute | solution.py:23
  72.2 34.5 %all-to-all-start = ((f32[1,2,8,128,128]{4,2,1,0,3:T(8,128)}), f32[1,2,8,128,128]{4,2,1,0,3:T(8,128)}, u32[]{:S(2)}, u32[]{:S(2)}) async-start(f32[1,2,8,128,128]{4,2,1,0,3:T(8,128)} %copy.35), calls=%async_computation | async-start | bytes 2097152 | tf_op jit(solution)/shard_map/all_to_all | solution.py:97
  80.3 3.5 %copy-start = (f32[1,2,8,128,128]{4,3,2,1,0:T(8,128)S(1)}, f32[1,2,8,128,128]{4,3,2,1,0:T(8,128)}, u32[]{:S(2)}) copy-start(f32[1,2,8,128,128]{4,3,2,1,0:T(8,128)} %param.2) | copy-start | bytes 3145732
  106.6 31.4 %all-to-all-start.2 = ((f32[1,2,8,128,128]{4,2,1,0,3:T(8,128)}), f32[1,2,8,128,128]{4,2,1,0,3:T(8,128)}, u32[]{:S(2)}, u32[]{:S(2)}) async-start(f32[1,2,8,128,128]{4,2,1,0,3:T(8,128)} %copy.50), calls=%async_computation.2 | async-start | bytes 2097152 | tf_op jit(solution)/shard_map/all_to_all | solution.py:97
  138.0 2.0 copy-start.2
  138.0 2.0 copy-start.4
  143.5 31.4 %all-to-all-start.3 = ((f32[1,2,128,8,128]{4,3,1,0,2:T(8,128)}), f32[1,2,128,8,128]{4,3,1,0,2:T(8,128)S(1)}, u32[]{:S(2)}, u32[]{:S(2)}) async-start(f32[1,2,128,8,128]{4,3,1,0,2:T(8,128)} %copy.54), calls=%async_computation.3 | async-start | bytes 2097152 | tf_op jit(solution)/shard_map/all_to_all | solution.py:103
  174.9 31.5 %all-to-all-start.1 = ((f32[1,2,128,8,128]{4,3,1,0,2:T(8,128)}), f32[1,2,128,8,128]{4,3,1,0,2:T(8,128)}, u32[]{:S(2)}, u32[]{:S(2)}) async-start(f32[1,2,128,8,128]{4,3,1,0,2:T(8,128)} %copy.40), calls=%async_computation.1 | async-start | bytes 2097152 | tf_op jit(solution)/shard_map/all_to_all | solution.py:103
  206.4 2.0 copy-start.1
  206.4 2.0 copy-start.3

commit v5 on v0

--- a/solution.py
+++ b/solution.py
@@ -5,10 +5,10 @@
 from jax import lax
 from jax.sharding import PartitionSpec as P
 
+
 NX = 128
 NY = 128
 NZ = 128
-STEPS = 2
 
 
 fused_forms = {1: "prnbc,rntk->ptkbc", 2: "pranc,rntk->ptakc", 3: "prabn,rntk->ptabk"}
@@ -22,14 +22,14 @@
     def send(operand, pairs):
         return lax.ppermute(operand, axis, [(band_place(h, *a), band_place(h, *b)) for h in (0, 1) for a, b in pairs])
 
-    first = [send(value, [((0, 0), (0, 1))]), send(value, [((0, 0), (1, 0))]), send(value, [((0, 0), (3, 0))])]
-    relay = first[1] + first[2]
+    first = [send(value, [((0, 0), (1, 0))]), send(value, [((0, 0), (3, 0))]), send(value, [((0, 0), (0, 1))])]
+    relay = first[0] + first[1]
     second = [
-        send(relay, [((1, 0), (1, 1)), ((3, 0), (3, 1))]),
         send(relay, [((1, 0), (2, 0))]),
         send(relay, [((3, 0), (2, 1))]),
+        send(relay, [((1, 0), (1, 1)), ((3, 0), (3, 1))]),
     ]
-    total = first[0] + relay
+    total = first[2] + relay
     for part in second:
         total = total + part
     return total

time: 192 us -> 192 us (level)
  no operation moved by 1% of the time
where the time goes in v5:
time: 192 us; the launch traced here: 191 us
  waiting for transfers between devices  114 us (59%)
  starting transfers between devices  44.8 us (23%)
  matrix products  14.5 us (8%)
  other arithmetic  9.97 us (5%)
  local copies, waits for them, and re-layouts  7.43 us (4%)
    all_to_all x2, waiting for transfers between devices, body(): lax.all_to_all(stacked, 'grid', split_axis=3, concat_axis=2, tiled=True)  47 us
    all_to_all x2, waiting for transfers between devices, body(): lax.all_to_all(back, 'grid', split_axis=2, concat_axis=3, tiled=True)  36.8 us
    ppermute x12, waiting for transfers between devices, send(): lax.ppermute(operand, axis, [(band_place(h, *a), band_place(h, *b)) for h...  29.9 us
    all_to_all x2, starting transfers between devices, body(): lax.all_to_all(stacked, 'grid', split_axis=3, concat_axis=2, tiled=True)  18.9 us
    ppermute x12, starting transfers between devices, send(): lax.ppermute(operand, axis, [(band_place(h, *a), band_place(h, *b)) for h...  16 us
    dot_general x12, matrix products, transform(): jnp.einsum(fused_forms[axis_dim], values, table, precision=lax.Precision....  14.5 us
    all_to_all x2, starting transfers between devices, body(): lax.all_to_all(back, 'grid', split_axis=2, concat_axis=3, tiled=True)  8.17 us
    transpose x4, local copies, waits for them, and re-layouts, transform(): jnp.einsum(fused_forms[axis_dim], values, table, precision=lax.Precision....  6.34 us
  transfers between devices with their start and end apart: 17, of which 6 were waited for; matrix products, arithmetic and copies ran while one was open for 11% of the time, Pallas kernels for 0%

profile of v5, /device:TPU:24, one launch (start us, length us, event | category | flops | bytes accessed | tf_op | source)
XLA Modules:
  0.0 190.7 jit_solution(13443046109021078896)
XLA Ops:
  1.5 1.6 collective-permute-start.6
  7.9 18.3 %collective-permute-done.2 = f32[1,2,8,128,128]{4,3,1,2,0:T(8,128)S(1)} collective-permute-done((f32[1,2,8,128,128]{4,3,1,2,0:T(8,128)S(1)}, f32[1,2,8,128,128]{4,3,1,2,0:T(8,128)S(1)}, u32[]{:S(2)}, u32[]{:S(2)}) %collective-permute-start.2) | collective-permute-done | bytes 1048608 | tf_op jit(solution)/shard_map/ppermute | solution.py:23
  30.4 11.6 %collective-permute-done.9 = f32[1,2,8,128,128]{4,3,1,2,0:T(8,128)S(1)} collective-permute-done((f32[1,2,8,128,128]{4,3,1,2,0:T(8,128)}, f32[1,2,8,128,128]{4,3,1,2,0:T(8,128)S(1)}, u32[]{:S(2)}, u32[]{:S(2)}) %collective-permute-start.9) | collective-permute-done | bytes 1048608 | tf_op jit(solution)/shard_map/ppermute | solution.py:23
  42.0 1.6 collective-permute-start.7
  44.7 2.3 %collective-permute-start.12 = (f32[1,2,8,128,128]{4,3,1,2,0:T(8,128)}, f32[1,2,8,128,128]{4,3,1,2,0:T(8,128)}, u32[]{:S(2)}, u32[]{:S(2)}) collective-permute-start(f32[1,2,8,128,128]{4,3,1,2,0:T(8,128)} %add.131), channel_id=1, source_target_pairs={{32,48},{96,112},{160,176},{224,240},{33,49},{97,113},{161,177},{2... | collective-permute-start | bytes 3145736 | tf_op jit(solution)/shard_map/ppermute | solution.py:23
  47.0 2.3 %collective-permute-start.11 = (f32[1,2,8,128,128]{4,3,1,2,0:T(8,128)}, f32[1,2,8,128,128]{4,3,1,2,0:T(8,128)}, u32[]{:S(2)}, u32[]{:S(2)}) collective-permute-start(f32[1,2,8,128,128]{4,3,1,2,0:T(8,128)} %add.131), channel_id=1, source_target_pairs={{96,80},{224,208},{97,81},{225,209},{98,82},{226,210},{99,83},{227... | collective-permute-start | bytes 3145736 | tf_op jit(solution)/shard_map/ppermute | solution.py:23
  49.3 1.7 collective-permute-start.10
  52.9 1.6 copy.35
  54.5 14.6 %all-to-all-start = ((f32[1,2,8,128,128]{4,2,1,0,3:T(8,128)}), f32[1,2,8,128,128]{4,2,1,0,3:T(8,128)}, u32[]{:S(2)}, u32[]{:S(2)}) async-start(f32[1,2,8,128,128]{4,2,1,0,3:T(8,128)} %copy.35), calls=%async_computation | async-start | bytes 2097152 | tf_op jit(solution)/shard_map/all_to_all | solution.py:89
  69.2 3.4 %add_add_fusion = f32[1,2,8,128,128]{4,3,1,2,0:T(8,128)S(1)} fusion(f32[1,2,8,128,128]{4,3,1,2,0:T(8,128)} %collective-permute-done.6, f32[1,2,8,128,128]{4,3,1,2,0:T(8,128)} %collective-permute-done.12, f32[1,2,8,128,128]{4,3,1,2,0:T(8,128)} %collective-permute-done.11, f32[1,2,8,128,128]{4,3,1,2,0:T(8,128)} %collective-permute-done.10, ...), kind=kLoop, calls=%fused_computation.35 | loop fusion | flops 1310720 | bytes 7340032 | tf_op jit(solution)/shard_map/add | solution.py:43
  74.0 1.6 copy.50
  75.6 22.3 %all-to-all-done = f32[1,2,8,128,128]{4,2,1,0,3:T(8,128)} async-done(((f32[1,2,8,128,128]{4,2,1,0,3:T(8,128)}), f32[1,2,8,128,128]{4,2,1,0,3:T(8,128)}, u32[]{:S(2)}, u32[]{:S(2)}) %all-to-all-start) | async-done | bytes 1048608 | tf_op jit(solution)/shard_map/all_to_all | solution.py:89
  97.9 4.3 %all-to-all-start.2 = ((f32[1,2,8,128,128]{4,2,1,0,3:T(8,128)}), f32[1,2,8,128,128]{4,2,1,0,3:T(8,128)}, u32[]{:S(2)}, u32[]{:S(2)}) async-start(f32[1,2,8,128,128]{4,2,1,0,3:T(8,128)} %copy.50), calls=%async_computation.2 | async-start | bytes 2097152 | tf_op jit(solution)/shard_map/all_to_all | solution.py:89
  103.0 2.8 %convolution_bitcast_fusion.10 = f32[1,2,128,8,128]{4,2,3,1,0:T(8,128)} fusion(f32[1,2,8,16,8,128]{5,2,1,4,3,0:T(8,128)} %bitcast.23, f32[1,128,2,128]{1,3,0,2:T(8,128)S(1)} %get-tuple-element.26, f32[1,128,2,128]{1,3,0,2:T(8,128)S(1)} %get-tuple-element.29), kind=kOutput, calls=%fused_computation.10 | convolution fusion | flops 402718720 | bytes 2359296 | tf_op jit(solution)/shard_map/prnbc,rntk->ptkbc/dot_general | solution.py:58
  105.8 24.7 %all-to-all-done.2 = f32[1,2,8,128,128]{4,2,1,0,3:T(8,128)} async-done(((f32[1,2,8,128,128]{4,2,1,0,3:T(8,128)}), f32[1,2,8,128,128]{4,2,1,0,3:T(8,128)}, u32[]{:S(2)}, u32[]{:S(2)}) %all-to-all-start.2) | async-done | bytes 1048608 | tf_op jit(solution)/shard_map/all_to_all | solution.py:89
  130.5 2.0 %convolution_bitcast_fusion.5 = f32[1,2,128,8,128]{4,2,3,1,0:T(8,128)S(1)} fusion(f32[1,2,8,16,8,128]{5,2,1,4,3,0:T(8,128)} %bitcast.68, f32[1,128,2,128]{1,3,0,2:T(8,128)S(1)} %get-tuple-element.26, f32[1,128,2,128]{1,3,0,2:T(8,128)S(1)} %get-tuple-element.29), kind=kOutput, calls=%fused_computation.5 | convolution fusion | flops 402718720 | bytes 2359296 | tf_op jit(solution)/shard_map/prnbc,rntk->ptkbc/dot_general | solution.py:58
  135.9 3.8 %all-to-all-start.3 = ((f32[1,2,128,8,128]{4,3,1,0,2:T(8,128)}), f32[1,2,128,8,128]{4,3,1,0,2:T(8,128)S(1)}, u32[]{:S(2)}, u32[]{:S(2)}) async-start(f32[1,2,128,8,128]{4,3,1,0,2:T(8,128)} %copy.54), calls=%async_computation.3 | async-start | bytes 2097152 | tf_op jit(solution)/shard_map/all_to_all | solution.py:95
  139.8 1.8 convolution_bitcast_fusion.9
  141.6 1.6 copy.40
  143.2 20.5 %all-to-all-done.3 = f32[1,2,128,8,128]{4,3,1,0,2:T(8,128)S(1)} async-done(((f32[1,2,128,8,128]{4,3,1,0,2:T(8,128)}), f32[1,2,128,8,128]{4,3,1,0,2:T(8,128)S(1)}, u32[]{:S(2)}, u32[]{:S(2)}) %all-to-all-start.3) | async-done | bytes 1048608 | tf_op jit(solution)/shard_map/all_to_all | solution.py:95
  163.7 4.3 %all-to-all-start.1 = ((f32[1,2,128,8,128]{4,3,1,0,2:T(8,128)}), f32[1,2,128,8,128]{4,3,1,0,2:T(8,128)}, u32[]{:S(2)}, u32[]{:S(2)}) async-start(f32[1,2,128,8,128]{4,3,1,0,2:T(8,128)} %copy.40), calls=%async_computation.1 | async-start | bytes 2097152 | tf_op jit(solution)/shard_map/all_to_all | solution.py:95
  168.0 1.6 convolution_bitcast_fusion.3
  169.6 16.3 %all-to-all-done.1 = f32[1,2,128,8,128]{4,3,1,0,2:T(8,128)} async-done(((f32[1,2,128,8,128]{4,3,1,0,2:T(8,128)}), f32[1,2,128,8,128]{4,3,1,0,2:T(8,128)}, u32[]{:S(2)}, u32[]{:S(2)}) %all-to-all-start.1) | async-done | bytes 1048608 | tf_op jit(solution)/shard_map/all_to_all | solution.py:95
  186.0 1.9 %convolution_bitcast_fusion.8 = f32[2,8,128,128,1]{3,2,1,0,4:T(8,128)S(1)} fusion(f32[1,2,16,8,8,128]{5,4,1,3,2,0:T(8,128)} %bitcast.39, f32[2,128,2,128,1]{1,3,2,0,4:T(8,128)S(1)} %get-tuple-element.24), kind=kOutput, calls=%fused_computation.8 | convolution fusion | flops 402653184 | bytes 2359296 | tf_op jit(solution)/shard_map/pranc,rntk->ptakc/dot_general | solution.py:58
  (51 shorter events, 21.9 us)
Async XLA Ops:
  1.5 3.7 %collective-permute-start.6 = (f32[1,2,8,128,128]{4,3,1,2,0:T(8,128)S(1)}, f32[1,2,8,128,128]{4,3,1,2,0:T(8,128)}, u32[]{:S(2)}, u32[]{:S(2)}) collective-permute-start(f32[1,2,8,128,128]{4,3,1,2,0:T(8,128)S(1)} %get-tuple-element.20), channel_id=1, source_target_pairs={{0,128},{128,0},{1,129},{129,1},{2,130},{130,2},{3,131},{131,3},{4... | collective-permute-start | bytes 3145736 | tf_op jit(solution)/shard_map/ppermute | solution.py:42
  3.1 4.8 %collective-permute-start.1 = (f32[1,2,8,128,128]{4,3,1,2,0:T(8,128)S(1)}, f32[1,2,8,128,128]{4,3,1,2,0:T(8,128)S(1)}, u32[]{:S(2)}, u32[]{:S(2)}) collective-permute-start(f32[1,2,8,128,128]{4,3,1,2,0:T(8,128)S(1)} %get-tuple-element.19), channel_id=1, source_target_pairs={{0,32},{128,160},{1,33},{129,161},{2,34},{130,162},{3,35},{131,163... | collective-permute-start | bytes 3145736 | tf_op jit(solution)/shard_map/ppermute | solution.py:23
  3.8 22.4 %collective-permute-start.2 = (f32[1,2,8,128,128]{4,3,1,2,0:T(8,128)S(1)}, f32[1,2,8,128,128]{4,3,1,2,0:T(8,128)S(1)}, u32[]{:S(2)}, u32[]{:S(2)}) collective-permute-start(f32[1,2,8,128,128]{4,3,1,2,0:T(8,128)S(1)} %get-tuple-element.19), channel_id=1, source_target_pairs={{0,96},{128,224},{1,97},{129,225},{2,98},{130,226},{3,99},{131,227... | collective-permute-start | bytes 3145736 | tf_op jit(solution)/shard_map/ppermute | solution.py:23
  5.1 23.9 %collective-permute-start.8 = (f32[1,2,8,128,128]{4,3,1,2,0:T(8,128)}, f32[1,2,8,128,128]{4,3,1,2,0:T(8,128)S(1)}, u32[]{:S(2)}, u32[]{:S(2)}) collective-permute-start(f32[1,2,8,128,128]{4,3,1,2,0:T(8,128)} %collective-permute-done.6), channel_id=1, source_target_pairs={{0,32},{128,160},{1,33},{129,161},{2,34},{130,162},{3,35},{131,163... | collective-permute-start | bytes 3145736 | tf_op jit(solution)/shard_map/ppermute | solution.py:23
  5.9 36.1 %collective-permute-start.9 = (f32[1,2,8,128,128]{4,3,1,2,0:T(8,128)}, f32[1,2,8,128,128]{4,3,1,2,0:T(8,128)S(1)}, u32[]{:S(2)}, u32[]{:S(2)}) collective-permute-start(f32[1,2,8,128,128]{4,3,1,2,0:T(8,128)} %collective-permute-done.6), channel_id=1, source_target_pairs={{0,96},{128,224},{1,97},{129,225},{2,98},{130,226},{3,99},{131,227... | collective-permute-start | bytes 3145736 | tf_op jit(solution)/shard_map/ppermute | solution.py:23
  7.2 37.5 %collective-permute-start = (f32[1,2,8,128,128]{4,3,1,2,0:T(8,128)S(1)}, f32[1,2,8,128,128]{4,3,1,2,0:T(8,128)S(1)}, u32[]{:S(2)}, u32[]{:S(2)}) collective-permute-start(f32[1,2,8,128,128]{4,3,1,2,0:T(8,128)S(1)} %get-tuple-element.19), channel_id=1, source_target_pairs={{0,16},{128,144},{1,17},{129,145},{2,18},{130,146},{3,19},{131,147... | collective-permute-start | bytes 3145736 | tf_op jit(solution)/shard_map/ppermute | solution.py:23
  26.3 20.6 %collective-permute-start.5 = (f32[1,2,8,128,128]{4,3,1,2,0:T(8,128)S(1)}, f32[1,2,8,128,128]{4,3,1,2,0:T(8,128)S(1)}, u32[]{:S(2)}, u32[]{:S(2)}) collective-permute-start(f32[1,2,8,128,128]{4,3,1,2,0:T(8,128)S(1)} %add.124), channel_id=1, source_target_pairs={{32,48},{96,112},{160,176},{224,240},{33,49},{97,113},{161,177},{2... | collective-permute-start | bytes 3145736 | tf_op jit(solution)/shard_map/ppermute | solution.py:23
  27.7 21.6 %collective-permute-start.4 = (f32[1,2,8,128,128]{4,3,1,2,0:T(8,128)S(1)}, f32[1,2,8,128,128]{4,3,1,2,0:T(8,128)S(1)}, u32[]{:S(2)}, u32[]{:S(2)}) collective-permute-start(f32[1,2,8,128,128]{4,3,1,2,0:T(8,128)S(1)} %add.124), channel_id=1, source_target_pairs={{96,80},{224,208},{97,81},{225,209},{98,82},{226,210},{99,83},{227... | collective-permute-start | bytes 3145736 | tf_op jit(solution)/shard_map/ppermute | solution.py:23
  29.1 21.8 %collective-permute-start.3 = (f32[1,2,8,128,128]{4,3,1,2,0:T(8,128)S(1)}, f32[1,2,8,128,128]{4,3,1,2,0:T(8,128)S(1)}, u32[]{:S(2)}, u32[]{:S(2)}) collective-permute-start(f32[1,2,8,128,128]{4,3,1,2,0:T(8,128)S(1)} %add.124), channel_id=1, source_target_pairs={{32,64},{160,192},{33,65},{161,193},{34,66},{162,194},{35,67},{163... | collective-permute-start | bytes 3145736 | tf_op jit(solution)/shard_map/ppermute | solution.py:23
  42.0 27.1 %collective-permute-start.7 = (f32[1,2,8,128,128]{4,3,1,2,0:T(8,128)}, f32[1,2,8,128,128]{4,3,1,2,0:T(8,128)}, u32[]{:S(2)}, u32[]{:S(2)}) collective-permute-start(f32[1,2,8,128,128]{4,3,1,2,0:T(8,128)} %collective-permute-done.6), channel_id=1, source_target_pairs={{0,16},{128,144},{1,17},{129,145},{2,18},{130,146},{3,19},{131,147... | collective-permute-start | bytes 3145736 | tf_op jit(solution)/shard_map/ppermute | solution.py:23
  44.7 24.4 %collective-permute-start.12 = (f32[1,2,8,128,128]{4,3,1,2,0:T(8,128)}, f32[1,2,8,128,128]{4,3,1,2,0:T(8,128)}, u32[]{:S(2)}, u32[]{:S(2)}) collective-permute-start(f32[1,2,8,128,128]{4,3,1,2,0:T(8,128)} %add.131), channel_id=1, source_target_pairs={{32,48},{96,112},{160,176},{224,240},{33,49},{97,113},{161,177},{2... | collective-permute-start | bytes 3145736 | tf_op jit(solution)/shard_map/ppermute | solution.py:23
  47.0 22.2 %collective-permute-start.11 = (f32[1,2,8,128,128]{4,3,1,2,0:T(8,128)}, f32[1,2,8,128,128]{4,3,1,2,0:T(8,128)}, u32[]{:S(2)}, u32[]{:S(2)}) collective-permute-start(f32[1,2,8,128,128]{4,3,1,2,0:T(8,128)} %add.131), channel_id=1, source_target_pairs={{96,80},{224,208},{97,81},{225,209},{98,82},{226,210},{99,83},{227... | collective-permute-start | bytes 3145736 | tf_op jit(solution)/shard_map/ppermute | solution.py:23
  49.3 19.9 %collective-permute-start.10 = (f32[1,2,8,128,128]{4,3,1,2,0:T(8,128)}, f32[1,2,8,128,128]{4,3,1,2,0:T(8,128)}, u32[]{:S(2)}, u32[]{:S(2)}) collective-permute-start(f32[1,2,8,128,128]{4,3,1,2,0:T(8,128)} %add.131), channel_id=1, source_target_pairs={{32,64},{160,192},{33,65},{161,193},{34,66},{162,194},{35,67},{163... | collective-permute-start | bytes 3145736 | tf_op jit(solution)/shard_map/ppermute | solution.py:23
  54.5 43.4 %all-to-all-start = ((f32[1,2,8,128,128]{4,2,1,0,3:T(8,128)}), f32[1,2,8,128,128]{4,2,1,0,3:T(8,128)}, u32[]{:S(2)}, u32[]{:S(2)}) async-start(f32[1,2,8,128,128]{4,2,1,0,3:T(8,128)} %copy.35), calls=%async_computation | async-start | bytes 2097152 | tf_op jit(solution)/shard_map/all_to_all | solution.py:89
  69.1 3.5 %copy-start = (f32[1,2,8,128,128]{4,3,2,1,0:T(8,128)S(1)}, f32[1,2,8,128,128]{4,3,2,1,0:T(8,128)}, u32[]{:S(2)}) copy-start(f32[1,2,8,128,128]{4,3,2,1,0:T(8,128)} %param.2) | copy-start | bytes 3145732
  97.9 32.5 %all-to-all-start.2 = ((f32[1,2,8,128,128]{4,2,1,0,3:T(8,128)}), f32[1,2,8,128,128]{4,2,1,0,3:T(8,128)}, u32[]{:S(2)}, u32[]{:S(2)}) async-start(f32[1,2,8,128,128]{4,2,1,0,3:T(8,128)} %copy.50), calls=%async_computation.2 | async-start | bytes 2097152 | tf_op jit(solution)/shard_map/all_to_all | solution.py:89
  130.5 2.0 %copy-start.2 = (f32[1,2,128,8,128]{4,2,3,1,0:T(8,128)S(1)}, f32[1,2,128,8,128]{4,2,3,1,0:T(8,128)}, u32[]{:S(2)}) copy-start(f32[1,2,128,8,128]{4,2,3,1,0:T(8,128)} %convolution_bitcast_fusion.10) | copy-start | bytes 3145732
  130.5 2.0 %copy-start.4 = (f32[128,8,128]{2,1,0:T(8,128)S(1)}, f32[128,8,128]{2,1,0:T(8,128)}, u32[]{:S(2)}) copy-start(f32[128,8,128]{2,1,0:T(8,128)} %param.3) | copy-start | bytes 1572868
  135.9 27.7 %all-to-all-start.3 = ((f32[1,2,128,8,128]{4,3,1,0,2:T(8,128)}), f32[1,2,128,8,128]{4,3,1,0,2:T(8,128)S(1)}, u32[]{:S(2)}, u32[]{:S(2)}) async-start(f32[1,2,128,8,128]{4,3,1,0,2:T(8,128)} %copy.54), calls=%async_computation.3 | async-start | bytes 2097152 | tf_op jit(solution)/shard_map/all_to_all | solution.py:95
  163.7 22.3 %all-to-all-start.1 = ((f32[1,2,128,8,128]{4,3,1,0,2:T(8,128)}), f32[1,2,128,8,128]{4,3,1,0,2:T(8,128)}, u32[]{:S(2)}, u32[]{:S(2)}) async-start(f32[1,2,128,8,128]{4,3,1,0,2:T(8,128)} %copy.40), calls=%async_computation.1 | async-start | bytes 2097152 | tf_op jit(solution)/shard_map/all_to_all | solution.py:95
  185.9 2.0 %copy-start.1 = (f32[2,8,128,128,1]{3,2,1,0,4:T(8,128)S(1)}, f32[2,8,128,128,1]{3,2,1,0,4:T(8,128)}, u32[]{:S(2)}) copy-start(f32[2,8,128,128,1]{3,2,1,0,4:T(8,128)} %convolution_bitcast_fusion.3) | copy-start | bytes 3145732
  186.0 2.0 %copy-start.3 = (f32[2,128,2,128]{1,3,2,0:T(8,128)S(1)}, f32[2,128,2,128]{1,3,2,0:T(8,128)}, u32[]{:S(2)}) copy-start(f32[2,128,2,128]{1,3,2,0:T(8,128)} %get-tuple-element.23) | copy-start | bytes 786436

commit v6 on v0

--- a/solution.py
+++ b/solution.py
@@ -5,10 +5,10 @@
 from jax import lax
 from jax.sharding import PartitionSpec as P
 
+
 NX = 128
 NY = 128
 NZ = 128
-STEPS = 2
 
 
 fused_forms = {1: "prnbc,rntk->ptkbc", 2: "pranc,rntk->ptakc", 3: "prabn,rntk->ptabk"}
@@ -61,7 +61,7 @@
 
 def body(bands, coulomb):
     local = bands.shape[0]
-    kernel = coulomb * (1.0 / (NX * NY * NZ))
+    kernel = coulomb * (-0.25 / (NX * NY * NZ))
     own_re = bands[:, 0]
     own_im = bands[:, 1]
     totals = (jnp.zeros_like(own_re), jnp.zeros_like(own_im))
@@ -88,8 +88,9 @@
         stacked = jnp.stack([potentials_real_part, potentials_imag_part], axis=1)
         block = lax.all_to_all(stacked, "grid", split_axis=3, concat_axis=2, tiled=True)
         pencil_real_part, pencil_imag_part = transform(block[:, 0], block[:, 1], 1, False)
-        pencil_real_part = pencil_real_part * kernel[None]
-        pencil_imag_part = pencil_imag_part * kernel[None]
+        pair_kernel, _ = lax.optimization_barrier((kernel, block))
+        pencil_real_part = pencil_real_part * pair_kernel[None]
+        pencil_imag_part = pencil_imag_part * pair_kernel[None]
         pencil_real_part, pencil_imag_part = transform(pencil_real_part, pencil_imag_part, 1, True)
         back = jnp.stack([pencil_real_part, pencil_imag_part], axis=1)
         result = lax.all_to_all(back, "grid", split_axis=2, concat_axis=3, tiled=True)
@@ -105,7 +106,7 @@
         add_re = jnp.sum(accumulate_pot_re * vis_re - accumulate_pot_im * vis_im, axis=1)
         add_im = jnp.sum(accumulate_pot_re * vis_im + accumulate_pot_im * vis_re, axis=1)
         totals = (totals[0] + add_re, totals[1] + add_im)
-    return -0.25 * jnp.stack([totals[0], totals[1]], axis=1)
+    return jnp.stack([totals[0], totals[1]], axis=1)
 
 
 def solution(mesh):

time: 192 us -> 192 us (level)
  no operation moved by 1% of the time
where the time goes in v6:
time: 192 us; the launch traced here: 190 us
  waiting for transfers between devices  112 us (58%)
  starting transfers between devices  44.8 us (23%)
  matrix products  14.5 us (8%)
  other arithmetic  11.1 us (6%)
  local copies, waits for them, and re-layouts  7.43 us (4%)
    all_to_all x2, waiting for transfers between devices, body(): lax.all_to_all(stacked, 'grid', split_axis=3, concat_axis=2, tiled=True)  44.5 us
    all_to_all x2, waiting for transfers between devices, body(): lax.all_to_all(back, 'grid', split_axis=2, concat_axis=3, tiled=True)  37.7 us
    ppermute x12, waiting for transfers between devices, send(): lax.ppermute(operand, axis, [(band_place(h, *a), band_place(h, *b)) for h...  29.9 us
    all_to_all x2, starting transfers between devices, body(): lax.all_to_all(stacked, 'grid', split_axis=3, concat_axis=2, tiled=True)  18.9 us
    ppermute x12, starting transfers between devices, send(): lax.ppermute(operand, axis, [(band_place(h, *a), band_place(h, *b)) for h...  16 us
    dot_general x12, matrix products, transform(): jnp.einsum(fused_forms[axis_dim], values, table, precision=lax.Precision....  14.5 us
    all_to_all x2, starting transfers between devices, body(): lax.all_to_all(back, 'grid', split_axis=2, concat_axis=3, tiled=True)  8.19 us
    transpose x4, local copies, waits for them, and re-layouts, transform(): jnp.einsum(fused_forms[axis_dim], values, table, precision=lax.Precision....  6.35 us
  transfers between devices with their start and end apart: 17, of which 6 were waited for; matrix products, arithmetic and copies ran while one was open for 11% of the time, Pallas kernels for 0%

profile of v6, /device:TPU:24, one launch (start us, length us, event | category | flops | bytes accessed | tf_op | source)
XLA Modules:
  0.0 190.1 jit_solution(2695945946737754938)
XLA Ops:
  1.5 1.6 collective-permute-start.6
  7.9 18.3 %collective-permute-done.2 = f32[1,2,8,128,128]{4,3,1,2,0:T(8,128)S(1)} collective-permute-done((f32[1,2,8,128,128]{4,3,1,2,0:T(8,128)S(1)}, f32[1,2,8,128,128]{4,3,1,2,0:T(8,128)S(1)}, u32[]{:S(2)}, u32[]{:S(2)}) %collective-permute-start.2) | collective-permute-done | bytes 1048608 | tf_op jit(solution)/shard_map/ppermute | solution.py:23
  30.4 11.6 %collective-permute-done.9 = f32[1,2,8,128,128]{4,3,1,2,0:T(8,128)S(1)} collective-permute-done((f32[1,2,8,128,128]{4,3,1,2,0:T(8,128)}, f32[1,2,8,128,128]{4,3,1,2,0:T(8,128)S(1)}, u32[]{:S(2)}, u32[]{:S(2)}) %collective-permute-start.9) | collective-permute-done | bytes 1048608 | tf_op jit(solution)/shard_map/ppermute | solution.py:23
  42.0 1.6 collective-permute-start.7
  44.7 2.3 %collective-permute-start.12 = (f32[1,2,8,128,128]{4,3,1,2,0:T(8,128)}, f32[1,2,8,128,128]{4,3,1,2,0:T(8,128)}, u32[]{:S(2)}, u32[]{:S(2)}) collective-permute-start(f32[1,2,8,128,128]{4,3,1,2,0:T(8,128)} %add.131), channel_id=1, source_target_pairs={{96,80},{224,208},{97,81},{225,209},{98,82},{226,210},{99,83},{227... | collective-permute-start | bytes 3145736 | tf_op jit(solution)/shard_map/ppermute | solution.py:23
  47.0 1.7 collective-permute-start.11
  48.6 2.3 %collective-permute-start.10 = (f32[1,2,8,128,128]{4,3,1,2,0:T(8,128)}, f32[1,2,8,128,128]{4,3,1,2,0:T(8,128)}, u32[]{:S(2)}, u32[]{:S(2)}) collective-permute-start(f32[1,2,8,128,128]{4,3,1,2,0:T(8,128)} %add.131), channel_id=1, source_target_pairs={{32,48},{96,112},{160,176},{224,240},{33,49},{97,113},{161,177},{2... | collective-permute-start | bytes 3145736 | tf_op jit(solution)/shard_map/ppermute | solution.py:23
  54.5 14.6 %all-to-all-start = ((f32[1,2,8,128,128]{4,2,1,0,3:T(8,128)}), f32[1,2,8,128,128]{4,2,1,0,3:T(8,128)}, u32[]{:S(2)}, u32[]{:S(2)}) async-start(f32[1,2,8,128,128]{4,2,1,0,3:T(8,128)} %copy.35), calls=%async_computation | async-start | bytes 2097152 | tf_op jit(solution)/shard_map/all_to_all | solution.py:89
  69.2 3.4 %add_add_fusion = f32[1,2,8,128,128]{4,3,1,2,0:T(8,128)S(1)} fusion(f32[1,2,8,128,128]{4,3,1,2,0:T(8,128)} %collective-permute-done.6, f32[1,2,8,128,128]{4,3,1,2,0:T(8,128)} %collective-permute-done.12, f32[1,2,8,128,128]{4,3,1,2,0:T(8,128)} %collective-permute-done.11, f32[1,2,8,128,128]{4,3,1,2,0:T(8,128)} %collective-permute-done.10, ...), kind=kLoop, calls=%fused_computation.35 | loop fusion | flops 1310720 | bytes 7340032 | tf_op jit(solution)/shard_map/add | solution.py:43
  74.0 1.6 copy.50
  75.6 21.8 %all-to-all-done = f32[1,2,8,128,128]{4,2,1,0,3:T(8,128)} async-done(((f32[1,2,8,128,128]{4,2,1,0,3:T(8,128)}), f32[1,2,8,128,128]{4,2,1,0,3:T(8,128)}, u32[]{:S(2)}, u32[]{:S(2)}) %all-to-all-start) | async-done | bytes 1048608 | tf_op jit(solution)/shard_map/all_to_all | solution.py:89
  97.4 4.3 %all-to-all-start.2 = ((f32[1,2,8,128,128]{4,2,1,0,3:T(8,128)}), f32[1,2,8,128,128]{4,2,1,0,3:T(8,128)}, u32[]{:S(2)}, u32[]{:S(2)}) async-start(f32[1,2,8,128,128]{4,2,1,0,3:T(8,128)} %copy.50), calls=%async_computation.2 | async-start | bytes 2097152 | tf_op jit(solution)/shard_map/all_to_all | solution.py:89
  103.6 2.8 %convolution_bitcast_fusion.10 = f32[1,2,128,8,128]{4,2,3,1,0:T(8,128)} fusion(f32[1,2,8,16,8,128]{5,2,1,4,3,0:T(8,128)} %bitcast.23, f32[1,128,2,128]{1,3,0,2:T(8,128)S(1)} %get-tuple-element.26, f32[1,128,2,128]{1,3,0,2:T(8,128)S(1)} %get-tuple-element.29), kind=kOutput, calls=%fused_computation.10 | convolution fusion | flops 402718720 | bytes 2359296 | tf_op jit(solution)/shard_map/prnbc,rntk->ptkbc/dot_general | solution.py:58
  106.4 22.7 %all-to-all-done.2 = f32[1,2,8,128,128]{4,2,1,0,3:T(8,128)} async-done(((f32[1,2,8,128,128]{4,2,1,0,3:T(8,128)}), f32[1,2,8,128,128]{4,2,1,0,3:T(8,128)}, u32[]{:S(2)}, u32[]{:S(2)}) %all-to-all-start.2) | async-done | bytes 1048608 | tf_op jit(solution)/shard_map/all_to_all | solution.py:89
  129.1 1.9 %convolution_bitcast_fusion.5 = f32[1,2,128,8,128]{4,2,3,1,0:T(8,128)S(1)} fusion(f32[1,2,8,16,8,128]{5,2,1,4,3,0:T(8,128)} %bitcast.68, f32[1,128,2,128]{1,3,0,2:T(8,128)S(1)} %get-tuple-element.26, f32[1,128,2,128]{1,3,0,2:T(8,128)S(1)} %get-tuple-element.29), kind=kOutput, calls=%fused_computation.5 | convolution fusion | flops 402718720 | bytes 2359296 | tf_op jit(solution)/shard_map/prnbc,rntk->ptkbc/dot_general | solution.py:58
  132.9 1.6 copy.54
  134.5 3.8 %all-to-all-start.3 = ((f32[1,2,128,8,128]{4,3,1,0,2:T(8,128)}), f32[1,2,128,8,128]{4,3,1,0,2:T(8,128)S(1)}, u32[]{:S(2)}, u32[]{:S(2)}) async-start(f32[1,2,128,8,128]{4,3,1,0,2:T(8,128)} %copy.54), calls=%async_computation.3 | async-start | bytes 2097152 | tf_op jit(solution)/shard_map/all_to_all | solution.py:96
  138.4 1.8 convolution_bitcast_fusion.9
  140.2 1.6 copy.40
  141.8 21.3 %all-to-all-done.3 = f32[1,2,128,8,128]{4,3,1,0,2:T(8,128)S(1)} async-done(((f32[1,2,128,8,128]{4,3,1,0,2:T(8,128)}), f32[1,2,128,8,128]{4,3,1,0,2:T(8,128)S(1)}, u32[]{:S(2)}, u32[]{:S(2)}) %all-to-all-start.3) | async-done | bytes 1048608 | tf_op jit(solution)/shard_map/all_to_all | solution.py:96
  163.1 4.4 %all-to-all-start.1 = ((f32[1,2,128,8,128]{4,3,1,0,2:T(8,128)}), f32[1,2,128,8,128]{4,3,1,0,2:T(8,128)}, u32[]{:S(2)}, u32[]{:S(2)}) async-start(f32[1,2,128,8,128]{4,3,1,0,2:T(8,128)} %copy.40), calls=%async_computation.1 | async-start | bytes 2097152 | tf_op jit(solution)/shard_map/all_to_all | solution.py:96
  167.5 1.6 convolution_bitcast_fusion.3
  169.0 16.3 %all-to-all-done.1 = f32[1,2,128,8,128]{4,3,1,0,2:T(8,128)} async-done(((f32[1,2,128,8,128]{4,3,1,0,2:T(8,128)}), f32[1,2,128,8,128]{4,3,1,0,2:T(8,128)}, u32[]{:S(2)}, u32[]{:S(2)}) %all-to-all-start.1) | async-done | bytes 1048608 | tf_op jit(solution)/shard_map/all_to_all | solution.py:96
  185.4 1.9 %convolution_bitcast_fusion.8 = f32[2,8,128,128,1]{3,2,1,0,4:T(8,128)S(1)} fusion(f32[1,2,16,8,8,128]{5,4,1,3,2,0:T(8,128)} %bitcast.39, f32[2,128,2,128,1]{1,3,2,0,4:T(8,128)S(1)} %get-tuple-element.24), kind=kOutput, calls=%fused_computation.8 | convolution fusion | flops 402653184 | bytes 2359296 | tf_op jit(solution)/shard_map/pranc,rntk->ptakc/dot_general | solution.py:58
  (50 shorter events, 22.9 us)
Async XLA Ops:
  1.5 3.7 %collective-permute-start.6 = (f32[1,2,8,128,128]{4,3,1,2,0:T(8,128)S(1)}, f32[1,2,8,128,128]{4,3,1,2,0:T(8,128)}, u32[]{:S(2)}, u32[]{:S(2)}) collective-permute-start(f32[1,2,8,128,128]{4,3,1,2,0:T(8,128)S(1)} %get-tuple-element.20), channel_id=1, source_target_pairs={{0,128},{128,0},{1,129},{129,1},{2,130},{130,2},{3,131},{131,3},{4... | collective-permute-start | bytes 3145736 | tf_op jit(solution)/shard_map/ppermute | solution.py:42
  3.1 4.8 %collective-permute-start.1 = (f32[1,2,8,128,128]{4,3,1,2,0:T(8,128)S(1)}, f32[1,2,8,128,128]{4,3,1,2,0:T(8,128)S(1)}, u32[]{:S(2)}, u32[]{:S(2)}) collective-permute-start(f32[1,2,8,128,128]{4,3,1,2,0:T(8,128)S(1)} %get-tuple-element.19), channel_id=1, source_target_pairs={{0,32},{128,160},{1,33},{129,161},{2,34},{130,162},{3,35},{131,163... | collective-permute-start | bytes 3145736 | tf_op jit(solution)/shard_map/ppermute | solution.py:23
  3.8 22.4 %collective-permute-start.2 = (f32[1,2,8,128,128]{4,3,1,2,0:T(8,128)S(1)}, f32[1,2,8,128,128]{4,3,1,2,0:T(8,128)S(1)}, u32[]{:S(2)}, u32[]{:S(2)}) collective-permute-start(f32[1,2,8,128,128]{4,3,1,2,0:T(8,128)S(1)} %get-tuple-element.19), channel_id=1, source_target_pairs={{0,96},{128,224},{1,97},{129,225},{2,98},{130,226},{3,99},{131,227... | collective-permute-start | bytes 3145736 | tf_op jit(solution)/shard_map/ppermute | solution.py:23
  5.1 23.3 %collective-permute-start.8 = (f32[1,2,8,128,128]{4,3,1,2,0:T(8,128)}, f32[1,2,8,128,128]{4,3,1,2,0:T(8,128)S(1)}, u32[]{:S(2)}, u32[]{:S(2)}) collective-permute-start(f32[1,2,8,128,128]{4,3,1,2,0:T(8,128)} %collective-permute-done.6), channel_id=1, source_target_pairs={{0,32},{128,160},{1,33},{129,161},{2,34},{130,162},{3,35},{131,163... | collective-permute-start | bytes 3145736 | tf_op jit(solution)/shard_map/ppermute | solution.py:23
  5.9 36.1 %collective-permute-start.9 = (f32[1,2,8,128,128]{4,3,1,2,0:T(8,128)}, f32[1,2,8,128,128]{4,3,1,2,0:T(8,128)S(1)}, u32[]{:S(2)}, u32[]{:S(2)}) collective-permute-start(f32[1,2,8,128,128]{4,3,1,2,0:T(8,128)} %collective-permute-done.6), channel_id=1, source_target_pairs={{0,96},{128,224},{1,97},{129,225},{2,98},{130,226},{3,99},{131,227... | collective-permute-start | bytes 3145736 | tf_op jit(solution)/shard_map/ppermute | solution.py:23
  7.2 37.5 %collective-permute-start = (f32[1,2,8,128,128]{4,3,1,2,0:T(8,128)S(1)}, f32[1,2,8,128,128]{4,3,1,2,0:T(8,128)S(1)}, u32[]{:S(2)}, u32[]{:S(2)}) collective-permute-start(f32[1,2,8,128,128]{4,3,1,2,0:T(8,128)S(1)} %get-tuple-element.19), channel_id=1, source_target_pairs={{0,16},{128,144},{1,17},{129,145},{2,18},{130,146},{3,19},{131,147... | collective-permute-start | bytes 3145736 | tf_op jit(solution)/shard_map/ppermute | solution.py:23
  26.3 20.6 %collective-permute-start.5 = (f32[1,2,8,128,128]{4,3,1,2,0:T(8,128)S(1)}, f32[1,2,8,128,128]{4,3,1,2,0:T(8,128)S(1)}, u32[]{:S(2)}, u32[]{:S(2)}) collective-permute-start(f32[1,2,8,128,128]{4,3,1,2,0:T(8,128)S(1)} %add.124), channel_id=1, source_target_pairs={{96,80},{224,208},{97,81},{225,209},{98,82},{226,210},{99,83},{227... | collective-permute-start | bytes 3145736 | tf_op jit(solution)/shard_map/ppermute | solution.py:23
  27.7 20.9 %collective-permute-start.4 = (f32[1,2,8,128,128]{4,3,1,2,0:T(8,128)S(1)}, f32[1,2,8,128,128]{4,3,1,2,0:T(8,128)S(1)}, u32[]{:S(2)}, u32[]{:S(2)}) collective-permute-start(f32[1,2,8,128,128]{4,3,1,2,0:T(8,128)S(1)} %add.124), channel_id=1, source_target_pairs={{32,64},{160,192},{33,65},{161,193},{34,66},{162,194},{35,67},{163... | collective-permute-start | bytes 3145736 | tf_op jit(solution)/shard_map/ppermute | solution.py:23
  28.5 22.5 %collective-permute-start.3 = (f32[1,2,8,128,128]{4,3,1,2,0:T(8,128)S(1)}, f32[1,2,8,128,128]{4,3,1,2,0:T(8,128)S(1)}, u32[]{:S(2)}, u32[]{:S(2)}) collective-permute-start(f32[1,2,8,128,128]{4,3,1,2,0:T(8,128)S(1)} %add.124), channel_id=1, source_target_pairs={{32,48},{96,112},{160,176},{224,240},{33,49},{97,113},{161,177},{2... | collective-permute-start | bytes 3145736 | tf_op jit(solution)/shard_map/ppermute | solution.py:23
  42.0 27.1 %collective-permute-start.7 = (f32[1,2,8,128,128]{4,3,1,2,0:T(8,128)}, f32[1,2,8,128,128]{4,3,1,2,0:T(8,128)}, u32[]{:S(2)}, u32[]{:S(2)}) collective-permute-start(f32[1,2,8,128,128]{4,3,1,2,0:T(8,128)} %collective-permute-done.6), channel_id=1, source_target_pairs={{0,16},{128,144},{1,17},{129,145},{2,18},{130,146},{3,19},{131,147... | collective-permute-start | bytes 3145736 | tf_op jit(solution)/shard_map/ppermute | solution.py:23
  44.7 24.4 %collective-permute-start.12 = (f32[1,2,8,128,128]{4,3,1,2,0:T(8,128)}, f32[1,2,8,128,128]{4,3,1,2,0:T(8,128)}, u32[]{:S(2)}, u32[]{:S(2)}) collective-permute-start(f32[1,2,8,128,128]{4,3,1,2,0:T(8,128)} %add.131), channel_id=1, source_target_pairs={{96,80},{224,208},{97,81},{225,209},{98,82},{226,210},{99,83},{227... | collective-permute-start | bytes 3145736 | tf_op jit(solution)/shard_map/ppermute | solution.py:23
  47.0 22.2 %collective-permute-start.11 = (f32[1,2,8,128,128]{4,3,1,2,0:T(8,128)}, f32[1,2,8,128,128]{4,3,1,2,0:T(8,128)}, u32[]{:S(2)}, u32[]{:S(2)}) collective-permute-start(f32[1,2,8,128,128]{4,3,1,2,0:T(8,128)} %add.131), channel_id=1, source_target_pairs={{32,64},{160,192},{33,65},{161,193},{34,66},{162,194},{35,67},{163... | collective-permute-start | bytes 3145736 | tf_op jit(solution)/shard_map/ppermute | solution.py:23
  48.6 20.5 %collective-permute-start.10 = (f32[1,2,8,128,128]{4,3,1,2,0:T(8,128)}, f32[1,2,8,128,128]{4,3,1,2,0:T(8,128)}, u32[]{:S(2)}, u32[]{:S(2)}) collective-permute-start(f32[1,2,8,128,128]{4,3,1,2,0:T(8,128)} %add.131), channel_id=1, source_target_pairs={{32,48},{96,112},{160,176},{224,240},{33,49},{97,113},{161,177},{2... | collective-permute-start | bytes 3145736 | tf_op jit(solution)/shard_map/ppermute | solution.py:23
  54.5 42.8 %all-to-all-start = ((f32[1,2,8,128,128]{4,2,1,0,3:T(8,128)}), f32[1,2,8,128,128]{4,2,1,0,3:T(8,128)}, u32[]{:S(2)}, u32[]{:S(2)}) async-start(f32[1,2,8,128,128]{4,2,1,0,3:T(8,128)} %copy.35), calls=%async_computation | async-start | bytes 2097152 | tf_op jit(solution)/shard_map/all_to_all | solution.py:89
  69.1 3.5 %copy-start = (f32[1,2,8,128,128]{4,3,2,1,0:T(8,128)S(1)}, f32[1,2,8,128,128]{4,3,2,1,0:T(8,128)}, u32[]{:S(2)}) copy-start(f32[1,2,8,128,128]{4,3,2,1,0:T(8,128)} %param.2) | copy-start | bytes 3145732
  97.4 31.8 %all-to-all-start.2 = ((f32[1,2,8,128,128]{4,2,1,0,3:T(8,128)}), f32[1,2,8,128,128]{4,2,1,0,3:T(8,128)}, u32[]{:S(2)}, u32[]{:S(2)}) async-start(f32[1,2,8,128,128]{4,2,1,0,3:T(8,128)} %copy.50), calls=%async_computation.2 | async-start | bytes 2097152 | tf_op jit(solution)/shard_map/all_to_all | solution.py:89
  129.1 1.9 %copy-start.2 = (f32[1,2,128,8,128]{4,2,3,1,0:T(8,128)S(1)}, f32[1,2,128,8,128]{4,2,3,1,0:T(8,128)}, u32[]{:S(2)}) copy-start(f32[1,2,128,8,128]{4,2,3,1,0:T(8,128)} %convolution_bitcast_fusion.10) | copy-start | bytes 3145732
  134.5 28.6 %all-to-all-start.3 = ((f32[1,2,128,8,128]{4,3,1,0,2:T(8,128)}), f32[1,2,128,8,128]{4,3,1,0,2:T(8,128)S(1)}, u32[]{:S(2)}, u32[]{:S(2)}) async-start(f32[1,2,128,8,128]{4,3,1,0,2:T(8,128)} %copy.54), calls=%async_computation.3 | async-start | bytes 2097152 | tf_op jit(solution)/shard_map/all_to_all | solution.py:96
  163.1 22.3 %all-to-all-start.1 = ((f32[1,2,128,8,128]{4,3,1,0,2:T(8,128)}), f32[1,2,128,8,128]{4,3,1,0,2:T(8,128)}, u32[]{:S(2)}, u32[]{:S(2)}) async-start(f32[1,2,128,8,128]{4,3,1,0,2:T(8,128)} %copy.40), calls=%async_computation.1 | async-start | bytes 2097152 | tf_op jit(solution)/shard_map/all_to_all | solution.py:96
  185.4 2.0 %copy-start.1 = (f32[2,8,128,128,1]{3,2,1,0,4:T(8,128)S(1)}, f32[2,8,128,128,1]{3,2,1,0,4:T(8,128)}, u32[]{:S(2)}) copy-start(f32[2,8,128,128,1]{3,2,1,0,4:T(8,128)} %convolution_bitcast_fusion.3) | copy-start | bytes 3145732
  185.4 2.0 %copy-start.3 = (f32[2,128,2,128]{1,3,2,0:T(8,128)S(1)}, f32[2,128,2,128]{1,3,2,0:T(8,128)}, u32[]{:S(2)}) copy-start(f32[2,128,2,128]{1,3,2,0:T(8,128)} %get-tuple-element.23) | copy-start | bytes 786436
